TPU v7x, 128 devices: a whole 4x4x4 slice. The times are simulated.
128 devices in a mesh: ctx: 16 (over x, z_lo, core), ch: 8 (over z_hi, y).
Axes of the slice: x: 4, y: 4, z: 4 (z_hi: 2, z_lo: 2; z = z_hi * 2 + z_lo), core: 2. Of those that a mesh axis runs over, the one named last changes fastest.
Arguments:
- q_proj: bfloat16 [16384, 4096], P(('ctx', 'ch')), may hold values from -6 to 6
- k_proj: bfloat16 [16384, 4096], P(('ctx', 'ch')), may hold values from -6 to 6
- v_proj: bfloat16 [16384, 4096], P(('ctx', 'ch')), may hold values from -6 to 6
- filter_taps: bfloat16 [16384, 4096], P(('ctx', 'ch')), may hold values from -6 to 6
- out_grad: bfloat16 [16384, 4096], P(('ctx', 'ch')), may hold values from -6 to 6
Outputs:
- mixed: bfloat16 [16384, 4096], P(('ctx', 'ch'))
- q_grad: bfloat16 [16384, 4096], P(('ctx', 'ch'))
- k_grad: bfloat16 [16384, 4096], P(('ctx', 'ch'))
- v_grad: bfloat16 [16384, 4096], P(('ctx', 'ch'))
- filter_grad: bfloat16 [16384, 4096], P(('ctx', 'ch'))
All inputs are finite; a program needn't handle non-finite values.
Results may differ from a plain program's by a relative error of at most 0.013.
Values may be sent and summed in bfloat16 or wider, within the bound.
No kernel may reach another device: no remote copies, remote signals or barrier semaphores. Data moves between devices by JAX's collectives and lax.ppermute only.
A program may use at most 192 MiB of HBM per device.

v0:
```python
import math

import jax
import jax.numpy as jnp
from jax import lax
from jax.sharding import PartitionSpec as P

AXES = ("ctx", "ch")
F32 = jnp.float32
BF16 = jnp.bfloat16


def build_tables(first, second):
    points = first * second
    half = first // 2
    rows_first = jnp.arange(first, dtype=jnp.int32)
    rows_half = jnp.arange(half, dtype=jnp.int32)
    rows_second = jnp.arange(second, dtype=jnp.int32)
    outer_phase = rows_first[:, None] * rows_half[None, :] % first
    outer_angle = outer_phase.astype(F32) * (2.0 * math.pi / first)
    turn_phase = rows_first[:, None] * rows_second[None, :] % points
    turn_angle = turn_phase.astype(F32) * (2.0 * math.pi / points)
    inner_phase = rows_second[:, None] * rows_second[None, :] % second
    inner_angle = inner_phase.astype(F32) * (2.0 * math.pi / second)
    return (
        jnp.cos(outer_angle).astype(BF16),
        jnp.sin(outer_angle).astype(BF16),
        jnp.cos(turn_angle),
        jnp.sin(turn_angle),
        jnp.cos(inner_angle).astype(BF16),
        jnp.sin(inner_angle).astype(BF16),
    )


def mm(spec, left, right):
    return jnp.einsum(spec, left.astype(BF16), right.astype(BF16), preferred_element_type=F32)


def forward_spectrum(tables, signal):
    outer_cos, outer_sin, turn_cos, turn_sin, inner_cos, inner_sin = tables
    half = outer_cos.shape[1]
    second = inner_cos.shape[0]
    shaped = signal.reshape(signal.shape[0], half, second)
    real_outer = mm("kn,cnm->ckm", outer_cos, shaped)
    imag_outer = -mm("kn,cnm->ckm", outer_sin, shaped)
    real_turned = real_outer * turn_cos + imag_outer * turn_sin
    imag_turned = imag_outer * turn_cos - real_outer * turn_sin
    real_spec = mm("ckn,mn->ckm", real_turned, inner_cos) + mm("ckn,mn->ckm", imag_turned, inner_sin)
    imag_spec = mm("ckn,mn->ckm", imag_turned, inner_cos) - mm("ckn,mn->ckm", real_turned, inner_sin)
    return (real_spec, imag_spec)


def inverse_signal(tables, spec_pair, scale):
    outer_cos, outer_sin, turn_cos, turn_sin, inner_cos, inner_sin = tables
    real_spec, imag_spec = spec_pair
    real_inner = mm("ckn,mn->ckm", real_spec, inner_cos) - mm("ckn,mn->ckm", imag_spec, inner_sin)
    imag_inner = mm("ckn,mn->ckm", imag_spec, inner_cos) + mm("ckn,mn->ckm", real_spec, inner_sin)
    real_turned = (real_inner * turn_cos - imag_inner * turn_sin) * scale
    imag_turned = (imag_inner * turn_cos + real_inner * turn_sin) * scale
    result = mm("kn,ckm->cnm", outer_cos, real_turned) - mm("kn,ckm->cnm", outer_sin, imag_turned)
    return result.reshape(result.shape[0], -1)


def product(left_pair, right_pair):
    return (
        left_pair[0] * right_pair[0] - left_pair[1] * right_pair[1],
        left_pair[0] * right_pair[1] + left_pair[1] * right_pair[0],
    )


def product_conj(left_pair, right_pair):
    return (
        left_pair[0] * right_pair[0] + left_pair[1] * right_pair[1],
        left_pair[1] * right_pair[0] - left_pair[0] * right_pair[1],
    )


def to_channels(arrays):
    rows, width = arrays[0].shape
    devices = lax.psum(1, AXES)
    per_device = width // devices
    packed = jnp.concatenate([a.T.reshape(devices, per_device, rows) for a in arrays], axis=1)
    moved = lax.all_to_all(packed, AXES, split_axis=0, concat_axis=0, tiled=True)
    moved = moved.reshape(devices, len(arrays), per_device, rows).transpose(1, 2, 0, 3)
    return moved.reshape(len(arrays), per_device, devices * rows)


def to_tokens(cols):
    count, per_device, length = cols.shape
    devices = lax.psum(1, AXES)
    rows = length // devices
    packed = cols.reshape(count, per_device, devices, rows).transpose(2, 0, 1, 3)
    moved = lax.all_to_all(packed.reshape(devices, count * per_device, rows), AXES, split_axis=0, concat_axis=0, tiled=True)
    moved = moved.reshape(devices, count, per_device, rows).transpose(1, 3, 0, 2)
    return moved.reshape(count, rows, devices * per_device)


def body(q_proj, k_proj, v_proj, filter_taps, out_grad):
    query = q_proj.astype(F32)
    key = k_proj.astype(F32)
    value = v_proj.astype(F32)
    cotangent = out_grad.astype(F32)
    gated = (key * value).astype(BF16)
    back_in = (cotangent * query).astype(BF16)

    forward_in = to_channels([gated, filter_taps])
    gated_part, taps_part = forward_in[0], forward_in[1]
    length = gated_part.shape[1]
    points = 2 * length
    second = math.gcd(points, 128)
    first = points // second
    tables = build_tables(first, second)
    scale = 1.0 / (math.sqrt(length) * points)

    gated_spec = forward_spectrum(tables, gated_part)
    taps_spec = forward_spectrum(tables, taps_part)
    conv_out = inverse_signal(tables, product(taps_spec, gated_spec), scale)
    conv_back = to_tokens(conv_out.astype(BF16).reshape((1,) + conv_out.shape))[0].astype(F32)
    mixed = (query * conv_back).astype(BF16)
    q_grad = (cotangent * conv_back).astype(BF16)

    back_part = to_channels([back_in])[0]
    back_spec = forward_spectrum(tables, back_part)
    conv_grad = inverse_signal(tables, product_conj(back_spec, taps_spec), scale)
    filter_grad = inverse_signal(tables, product_conj(back_spec, gated_spec), scale)
    second_back = to_tokens(jnp.stack([conv_grad, filter_grad], 0).astype(BF16))
    grad_back = second_back[0].astype(F32)
    k_grad = (grad_back * value).astype(BF16)
    v_grad = (grad_back * key).astype(BF16)
    return (mixed, q_grad, k_grad, v_grad, second_back[1])


def solution(mesh):
    spec = P(AXES, None)
    return jax.shard_map(body, mesh=mesh, in_specs=(spec,) * 5, out_specs=(spec,) * 5, check_vma=False)
```

profile of v0, /device:TPU:0, one launch (start us, length us, event | category | flops | bytes accessed | tf_op | source)
XLA Modules:
  0.0 221.8 jit_solution(6485487168815499645)
XLA Ops:
  0.6 1.6 copy.118
  2.3 2.0 copy.138
  4.3 1.3 fusion.15
  5.6 11.7 %all-to-all-start.2 = ((bf16[128,32,128]{2,1,0:T(8,128)(2,1)}), bf16[128,32,128]{2,1,0:T(8,128)(2,1)}, u32[]{:S(2)}, u32[]{:S(2)}) async-start(bf16[128,32,128]{2,1,0:T(8,128)(2,1)} %bitcast.27), calls=%async_computation.2 | async-start | bytes 2097152 | tf_op jit(solution)/shard_map/all_to_all | solution.py:83
  17.3 1.6 copy.119
  18.9 1.6 copy.120
  20.6 2.6 %copy.121 = bf16[128,4096]{0,1:T(8,128)(2,1)} copy(bf16[128,4096]{1,0:T(8,128)(2,1)} %param.8) | data formatting | bytes 2097152 | tf_op args[3]
  23.5 2.9 %pad_maximum_fusion = bf16[128,64,128]{2,1,0:T(8,128)(2,1)} fusion(bf16[128,32,128]{2,1,0:T(8,128)(2,1)} %bitcast.200, bf16[128,32,128]{2,1,0:T(8,128)(2,1)S(1)} %bitcast.198), kind=kLoop, calls=%fused_computation.66 | loop fusion | flops 4194304 | bytes 4194304 | tf_op jit(solution)/shard_map/concatenate | solution.py:82
  26.4 9.9 %all-to-all-done.2 = bf16[128,32,128]{2,1,0:T(8,128)(2,1)} async-done(((bf16[128,32,128]{2,1,0:T(8,128)(2,1)}), bf16[128,32,128]{2,1,0:T(8,128)(2,1)}, u32[]{:S(2)}, u32[]{:S(2)}) %all-to-all-start.2) | async-done | bytes 1048608 | tf_op jit(solution)/shard_map/all_to_all | solution.py:83
  36.2 6.2 %all-to-all-start = ((bf16[128,64,128]{2,1,0:T(8,128)(2,1)}), bf16[128,64,128]{2,1,0:T(8,128)(2,1)}, u32[]{:S(2)}, u32[]{:S(2)}) async-start(bf16[128,64,128]{2,1,0:T(8,128)(2,1)} %pad_maximum_fusion), calls=%async_computation | async-start | bytes 4194304 | tf_op jit(solution)/shard_map/all_to_all | solution.py:83
  43.7 2.0 copy.139
  45.7 3.1 %fusion.45 = f32[32,128,256]{2,1,0:T(8,128)} fusion(bf16[128,32,128]{0,2,1:T(8,128)(2,1)S(1)} %copy.139), kind=kOutput, calls=%fused_computation.94 | convolution fusion | flops 268926976 | bytes 5242880 | tf_op jit(solution)/shard_map/kn,cnm->ckm/dot_general | solution.py:36
  48.8 23.9 %all-to-all-done = bf16[128,64,128]{2,1,0:T(8,128)(2,1)} async-done(((bf16[128,64,128]{2,1,0:T(8,128)(2,1)}), bf16[128,64,128]{2,1,0:T(8,128)(2,1)}, u32[]{:S(2)}, u32[]{:S(2)}) %all-to-all-start) | async-done | bytes 2097184 | tf_op jit(solution)/shard_map/all_to_all | solution.py:83
  72.6 3.3 %copy.122 = bf16[128,64,128]{0,2,1:T(8,128)(2,1)S(1)} copy(bf16[128,64,128]{2,1,0:T(8,128)(2,1)} %all-to-all-done) | data formatting | bytes 4194304 | tf_op jit(solution)/shard_map/all_to_all | solution.py:83
  75.9 3.2 %fusion.51 = f32[32,128,256]{2,1,0:T(8,128)} fusion(bf16[2,32,128,128]{2,3,1,0:T(8,128)(2,1)S(1)} %bitcast.193), kind=kOutput, calls=%fused_computation.100 | convolution fusion | flops 268926976 | bytes 5242880 | tf_op jit(solution)/shard_map/kn,cnm->ckm/dot_general | solution.py:36
  79.1 3.1 %fusion.49 = f32[32,128,256]{2,1,0:T(8,128)} fusion(bf16[2,32,128,128]{2,3,1,0:T(8,128)(2,1)S(1)} %bitcast.194), kind=kOutput, calls=%fused_computation.98 | convolution fusion | flops 268926976 | bytes 5242880 | tf_op jit(solution)/shard_map/kn,cnm->ckm/dot_general | solution.py:36
  82.2 3.1 %fusion.52 = f32[32,128,256]{2,1,0:T(8,128)} fusion(bf16[2,32,128,128]{2,3,1,0:T(8,128)(2,1)S(1)} %bitcast.195), kind=kOutput, calls=%fused_computation.101 | convolution fusion | flops 268926976 | bytes 5242880 | tf_op jit(solution)/shard_map/kn,cnm->ckm/dot_general | solution.py:36
  85.4 3.1 %fusion.50 = f32[32,128,256]{2,1,0:T(8,128)} fusion(bf16[2,32,128,128]{2,3,1,0:T(8,128)(2,1)S(1)} %bitcast.196), kind=kOutput, calls=%fused_computation.99 | convolution fusion | flops 268926976 | bytes 5242880 | tf_op jit(solution)/shard_map/kn,cnm->ckm/dot_general | solution.py:36
  88.5 9.6 %fusion.3 = (bf16[32,256,128]{1,2,0:T(8,128)(2,1)S(1)}, bf16[32,256,128]{1,2,0:T(8,128)(2,1)S(1)}, bf16[32,256,128]{1,2,0:T(8,128)(2,1)S(1)}, bf16[32,256,128]{1...) fusion(f32[32,128,256]{2,1,0:T(8,128)} %fusion.45, ...), kind=kOutput, calls=%fused_computation.5 | convolution fusion | flops 297238528 | bytes 34865152 | tf_op jit(solution)/shard_map/kn,cnm->ckm/dot_general | solution.py:36
  98.0 3.0 %fusion.108 = f32[32,256,128]{2,1,0:T(8,128)} fusion(bf16[32,256,128]{1,2,0:T(8,128)(2,1)S(1)} %get-tuple-element.26), kind=kOutput, calls=%fused_computation.142 | convolution fusion | flops 268681216 | bytes 6291456 | tf_op jit(solution)/shard_map/ckn,mn->ckm/dot_general | solution.py:36
  102.0 3.0 %convolution_add_fusion.2 = f32[32,256,128]{2,1,0:T(8,128)} fusion(f32[32,256,128]{2,1,0:T(8,128)S(1)} %fusion.110, bf16[32,256,128]{1,2,0:T(8,128)(2,1)S(1)} %get-tuple-element.26), kind=kOutput, calls=%fused_computation.47 | convolution fusion | flops 269729792 | bytes 10485760 | tf_op jit(solution)/shard_map/ckn,mn->ckm/dot_general | solution.py:36
  106.9 3.0 %convolution_add_fusion.4 = f32[32,256,128]{2,1,0:T(8,128)} fusion(f32[32,256,128]{2,1,0:T(8,128)S(1)} %fusion.120, bf16[32,256,128]{1,2,0:T(8,128)(2,1)S(1)} %get-tuple-element.43), kind=kOutput, calls=%fused_computation.52 | convolution fusion | flops 269729792 | bytes 10485760 | tf_op jit(solution)/shard_map/ckn,mn->ckm/dot_general | solution.py:36
  109.9 3.0 %convolution_subtract_fusion.4 = f32[32,256,128]{2,1,0:T(8,128)} fusion(f32[32,256,128]{2,1,0:T(8,128)S(1)} %fusion.116, bf16[32,256,128]{1,2,0:T(8,128)(2,1)S(1)} %get-tuple-element.42), kind=kOutput, calls=%fused_computation.50 | convolution fusion | flops 269729792 | bytes 10485760 | tf_op jit(solution)/shard_map/ckn,mn->ckm/dot_general | solution.py:36
  113.8 0.9 fusion.122
  114.8 2.9 %convolution_subtract_fusion.5 = f32[32,256,128]{2,1,0:T(8,128)} fusion(f32[32,256,128]{2,1,0:T(8,128)S(1)} %fusion.118, bf16[32,256,128]{1,2,0:T(8,128)(2,1)S(1)} %get-tuple-element.45), kind=kOutput, calls=%fused_computation.51 | convolution fusion | flops 269729792 | bytes 10485760 | tf_op jit(solution)/shard_map/ckn,mn->ckm/dot_general | solution.py:36
  117.7 2.9 %convolution_add_fusion.5 = f32[32,256,128]{2,1,0:T(8,128)} fusion(f32[32,256,128]{2,1,0:T(8,128)S(1)} %fusion.122, bf16[32,256,128]{1,2,0:T(8,128)(2,1)S(1)} %get-tuple-element.44), kind=kOutput, calls=%fused_computation.53 | convolution fusion | flops 269729792 | bytes 10485760 | tf_op jit(solution)/shard_map/ckn,mn->ckm/dot_general | solution.py:36
  120.6 12.3 %add_convert_fusion.1 = (bf16[32,256,128]{2,1,0:T(8,128)(2,1)S(1)}, bf16[32,256,128]{2,1,0:T(8,128)(2,1)S(1)}, bf16[32,256,128]{2,1,0:T(8,128)(2,1)S(1)}, bf16[3...) fusion(f32[32,256,128]{2,1,0:T(8,128)} %convolution_subtract_fusion.5, ...), kind=kOutput, calls=%fused_computation.31 | convolution fusion | flops 294895616 | bytes 39845888 | tf_op jit(solution)/shard_map/ckn,mn->ckm/dot_general | solution.py:36
  136.6 1.2 fusion.20
  137.8 2.3 %fusion.43 = bf16[1,32,128,128]{2,3,1,0:T(8,128)(2,1)} fusion(f32[32,128,128]{2,1,0:T(8,128)S(1)} %fusion.20, f32[32,256,128]{1,2,0:T(8,128)S(1)} %convolution_subtract_fusion.1, f32[32,256,128]{1,2,0:T(8,128)S(1)} %convolution_add_fusion.1, f32[256,128]{0,1:T(8,128)S(1)} %copy.124, f32[256,128]{0,1:T(8,128)S(1)} %copy.123), kind=kOutput, calls=%fused_computation.90 | convolution fusion | flops 275218432 | bytes 11796480 | tf_op jit(solution)/shard_map/kn,ckm->cnm/dot_general | solution.py:36
  143.8 1.2 fusion.18
  145.1 2.6 %fusion.42 = bf16[128,32,128]{0,2,1:T(8,128)(2,1)} fusion(f32[32,128,128]{2,1,0:T(8,128)S(1)} %fusion.18, f32[32,256,128]{1,2,0:T(8,128)S(1)} %convolution_subtract_fusion.3, f32[32,256,128]{1,2,0:T(8,128)S(1)} %convolution_add_fusion.3, f32[256,128]{0,1:T(8,128)S(1)} %copy.124, f32[256,128]{0,1:T(8,128)S(1)} %copy.123), kind=kOutput, calls=%fused_computation.89 | convolution fusion | flops 275218432 | bytes 11796480 | tf_op jit(solution)/shard_map/kn,ckm->cnm/dot_general | solution.py:36
  147.7 2.6 %copy.137 = bf16[128,32,128]{2,1,0:T(8,128)(2,1)} copy(bf16[128,32,128]{0,2,1:T(8,128)(2,1)} %fusion.42) | data formatting | bytes 2097152 | tf_op jit(solution)/shard_map/reshape | solution.py:93
  150.3 5.8 %all-to-all-start.1 = ((bf16[128,32,128]{2,1,0:T(8,128)(2,1)}), bf16[128,32,128]{2,1,0:T(8,128)(2,1)}, u32[]{:S(2)}, u32[]{:S(2)}) async-start(bf16[128,32,128]{2,1,0:T(8,128)(2,1)} %copy.137), calls=%async_computation.1 | async-start | bytes 2097152 | tf_op jit(solution)/shard_map/all_to_all | solution.py:93
  160.5 1.2 fusion.22
  161.7 1.4 fusion.44
  163.1 1.5 pad_maximum_fusion.1
  164.6 4.3 %copy.152 = bf16[128,64,128]{2,1,0:T(8,128)(2,1)} copy(bf16[128,64,128]{0,2,1:T(8,128)(2,1)} %bitcast.197) | data formatting | bytes 4194304 | tf_op jit(solution)/shard_map/reshape | solution.py:93
  168.9 6.1 %all-to-all-done.1 = bf16[128,32,128]{2,1,0:T(8,128)(2,1)} async-done(((bf16[128,32,128]{2,1,0:T(8,128)(2,1)}), bf16[128,32,128]{2,1,0:T(8,128)(2,1)}, u32[]{:S(2)}, u32[]{:S(2)}) %all-to-all-start.1) | async-done | bytes 1048608 | tf_op jit(solution)/shard_map/all_to_all | solution.py:93
  175.0 5.8 %all-to-all-start.3 = ((bf16[128,64,128]{2,1,0:T(8,128)(2,1)}), bf16[128,64,128]{2,1,0:T(8,128)(2,1)}, u32[]{:S(2)}, u32[]{:S(2)}) async-start(bf16[128,64,128]{2,1,0:T(8,128)(2,1)} %copy.152), calls=%async_computation.3 | async-start | bytes 4194304 | tf_op jit(solution)/shard_map/all_to_all | solution.py:93
  180.8 3.0 %fusion.14 = (bf16[128,4096]{0,1:T(8,128)(2,1)}, bf16[128,4096]{0,1:T(8,128)(2,1)}) fusion(bf16[128,4096]{0,1:T(8,128)(2,1)S(1)} %copy-done.6, bf16[128,32,128]{2,1,0:T(8,128)(2,1)} %all-to-all-done.1, bf16[128,4096]{0,1:T(8,128)(2,1)S(1)} %copy-done.4), kind=kLoop, calls=%fused_computation.56 | loop fusion | flops 3670016 | bytes 5242880 | tf_op jit(solution)/shard_map/convert_element_type | solution.py:120
  183.8 2.3 %copy.154 = bf16[128,4096]{1,0:T(8,128)(2,1)} copy(bf16[128,4096]{0,1:T(8,128)(2,1)} %get-tuple-element.40) | data formatting | bytes 2097152
  186.1 2.4 %copy.153 = bf16[128,4096]{1,0:T(8,128)(2,1)} copy(bf16[128,4096]{0,1:T(8,128)(2,1)} %get-tuple-element.41) | data formatting | bytes 2097152
  188.5 22.5 %all-to-all-done.3 = bf16[128,64,128]{2,1,0:T(8,128)(2,1)} async-done(((bf16[128,64,128]{2,1,0:T(8,128)(2,1)}), bf16[128,64,128]{2,1,0:T(8,128)(2,1)}, u32[]{:S(2)}, u32[]{:S(2)}) %all-to-all-start.3) | async-done | bytes 2097184 | tf_op jit(solution)/shard_map/all_to_all | solution.py:93
  211.0 2.9 %fusion.274 = (bf16[1,128,128,32]{1,3,0,2:T(8,128)(2,1)S(1)}, bf16[1,128,128,32]{1,3,0,2:T(8,128)(2,1)}) fusion(bf16[2,128,128,32]{1,3,0,2:T(8,128)(2,1)} %bitcast.42), kind=kLoop, calls=%fused_computation.300 | loop fusion | bytes 4194304 | tf_op jit(solution)/shard_map/slice | solution.py:130
  213.9 1.3 copy.157
  215.2 2.7 %fusion.17 = (bf16[128,4096]{0,1:T(8,128)(2,1)}, bf16[128,4096]{0,1:T(8,128)(2,1)S(1)}) fusion(bf16[128,4096]{0,1:T(8,128)(2,1)S(1)} %copy.119, bf16[1,128,128,32]{1,3,0,2:T(8,128)(2,1)} %get-tuple-element.37, bf16[128,4096]{0,1:T(8,128)(2,1)S(1)} %copy-done.2), kind=kLoop, calls=%fused_computation.59 | loop fusion | flops 3670016 | bytes 5242880 | tf_op jit(solution)/shard_map/convert_element_type | solution.py:129
  217.8 2.3 %copy.156 = bf16[128,4096]{1,0:T(8,128)(2,1)} copy(bf16[128,4096]{0,1:T(8,128)(2,1)} %get-tuple-element.38) | data formatting | bytes 2097152
  220.1 1.3 copy.155
  (41 shorter events, 16.9 us)
Async XLA Ops:
  2.3 15.0 %copy-start.3 = (bf16[128,4096]{0,1:T(8,128)(2,1)}, bf16[128,4096]{0,1:T(8,128)(2,1)S(1)}, u32[]{:S(2)}) copy-start(bf16[128,4096]{0,1:T(8,128)(2,1)S(1)} %copy.118) | copy-start | bytes 3145732
  4.3 16.3 %copy-start.5 = (bf16[128,4096]{0,1:T(8,128)(2,1)}, bf16[128,4096]{0,1:T(8,128)(2,1)S(1)}, u32[]{:S(2)}) copy-start(bf16[128,4096]{0,1:T(8,128)(2,1)S(1)} %copy.138) | copy-start | bytes 3145732
  5.6 30.6 %all-to-all-start.2 = ((bf16[128,32,128]{2,1,0:T(8,128)(2,1)}), bf16[128,32,128]{2,1,0:T(8,128)(2,1)}, u32[]{:S(2)}, u32[]{:S(2)}) async-start(bf16[128,32,128]{2,1,0:T(8,128)(2,1)} %bitcast.27), calls=%async_computation.2 | async-start | bytes 2097152 | tf_op jit(solution)/shard_map/all_to_all | solution.py:83
  20.6 5.8 %copy-start.1 = (bf16[128,4096]{0,1:T(8,128)(2,1)}, bf16[128,4096]{0,1:T(8,128)(2,1)S(1)}, u32[]{:S(2)}) copy-start(bf16[128,4096]{0,1:T(8,128)(2,1)S(1)} %copy.120) | copy-start | bytes 3145732
  36.2 36.4 %all-to-all-start = ((bf16[128,64,128]{2,1,0:T(8,128)(2,1)}), bf16[128,64,128]{2,1,0:T(8,128)(2,1)}, u32[]{:S(2)}, u32[]{:S(2)}) async-start(bf16[128,64,128]{2,1,0:T(8,128)(2,1)} %pad_maximum_fusion), calls=%async_computation | async-start | bytes 4194304 | tf_op jit(solution)/shard_map/all_to_all | solution.py:83
  45.6 3.1 %copy-start.7 = (bf16[128,32,128]{0,2,1:T(8,128)(2,1)}, bf16[128,32,128]{0,2,1:T(8,128)(2,1)S(1)}, u32[]{:S(2)}) copy-start(bf16[128,32,128]{0,2,1:T(8,128)(2,1)S(1)} %copy.139) | copy-start | bytes 3145732
  82.2 6.3 %copy-start.8 = (bf16[128,32,128]{0,2,1:T(8,128)(2,1)S(1)}, bf16[128,32,128]{0,2,1:T(8,128)(2,1)}, u32[]{:S(2)}) copy-start(bf16[128,32,128]{0,2,1:T(8,128)(2,1)} %copy-done.7) | copy-start | bytes 3145732
  150.3 24.7 %all-to-all-start.1 = ((bf16[128,32,128]{2,1,0:T(8,128)(2,1)}), bf16[128,32,128]{2,1,0:T(8,128)(2,1)}, u32[]{:S(2)}, u32[]{:S(2)}) async-start(bf16[128,32,128]{2,1,0:T(8,128)(2,1)} %copy.137), calls=%async_computation.1 | async-start | bytes 2097152 | tf_op jit(solution)/shard_map/all_to_all | solution.py:93
  156.1 1.6 copy-start
  161.7 1.4 copy-start.9
  164.6 16.2 %copy-start.4 = (bf16[128,4096]{0,1:T(8,128)(2,1)S(1)}, bf16[128,4096]{0,1:T(8,128)(2,1)}, u32[]{:S(2)}) copy-start(bf16[128,4096]{0,1:T(8,128)(2,1)} %copy-done.3) | copy-start | bytes 3145732
  164.6 16.2 %copy-start.6 = (bf16[128,4096]{0,1:T(8,128)(2,1)S(1)}, bf16[128,4096]{0,1:T(8,128)(2,1)}, u32[]{:S(2)}) copy-start(bf16[128,4096]{0,1:T(8,128)(2,1)} %copy-done.5) | copy-start | bytes 3145732
  175.0 35.9 %all-to-all-start.3 = ((bf16[128,64,128]{2,1,0:T(8,128)(2,1)}), bf16[128,64,128]{2,1,0:T(8,128)(2,1)}, u32[]{:S(2)}, u32[]{:S(2)}) async-start(bf16[128,64,128]{2,1,0:T(8,128)(2,1)} %copy.152), calls=%async_computation.3 | async-start | bytes 4194304 | tf_op jit(solution)/shard_map/all_to_all | solution.py:93
  186.1 29.1 %copy-start.2 = (bf16[128,4096]{0,1:T(8,128)(2,1)S(1)}, bf16[128,4096]{0,1:T(8,128)(2,1)}, u32[]{:S(2)}) copy-start(bf16[128,4096]{0,1:T(8,128)(2,1)} %copy-done.1) | copy-start | bytes 3145732
where the time goes:
time: 225 us; the launch traced here: 222 us
  matrix products  81 us (36%)
  waiting for transfers between devices  62.4 us (28%)
  local copies, waits for them, and re-layouts  35 us (16%)
  starting transfers between devices  29.5 us (13%)
  other arithmetic  12.6 us (6%)
    dot_general x36, matrix products, mm(): jnp.einsum(spec, left.astype(BF16), right.astype(BF16), preferred_element...  81 us
    all_to_all x2, waiting for transfers between devices, to_channels(): lax.all_to_all(packed, AXES, split_axis=0, concat_axis=0, tiled=True)  33.7 us
    all_to_all x2, waiting for transfers between devices, to_tokens(): lax.all_to_all(packed.reshape(devices, count * per_device, rows), AXES, s...  28.6 us
    unnamed x30, local copies, waits for them, and re-layouts  19.7 us
    all_to_all x2, starting transfers between devices, to_channels(): lax.all_to_all(packed, AXES, split_axis=0, concat_axis=0, tiled=True)  18 us
    all_to_all x2, starting transfers between devices, to_tokens(): lax.all_to_all(packed.reshape(devices, count * per_device, rows), AXES, s...  11.5 us
    reshape x2, local copies, waits for them, and re-layouts, to_tokens(): packed.reshape(devices, count * per_device, rows)  6.94 us
    all_to_all x2, local copies, waits for them, and re-layouts, to_channels(): lax.all_to_all(packed, AXES, split_axis=0, concat_axis=0, tiled=True)  5.25 us
  transfers between devices with their start and end apart: 4, of which 4 were waited for; matrix products, arithmetic and copies ran while one was open for 16% of the time, Pallas kernels for 0%

commit v1 on v0

--- a/solution.py
+++ b/solution.py
@@ -3,6 +3,8 @@
 import jax
 import jax.numpy as jnp
 from jax import lax
+from jax.experimental import pallas as pl
+from jax.experimental.pallas import tpu as pltpu
 from jax.sharding import PartitionSpec as P
 
 AXES = ("ctx", "ch")
@@ -95,6 +97,83 @@
     return moved.reshape(count, rows, devices * per_device)
 
 
+def kernel_tables(first, second):
+    outer_cos, outer_sin, turn_cos, turn_sin, inner_cos, inner_sin = build_tables(first, second)
+    stage_one = jnp.concatenate([outer_cos, -outer_sin], axis=0)
+    forward_two = jnp.concatenate(
+        [jnp.concatenate([inner_cos, -inner_sin], axis=1), jnp.concatenate([inner_sin, inner_cos], axis=1)], axis=0
+    )
+    inverse_two = jnp.concatenate(
+        [jnp.concatenate([inner_cos, inner_sin], axis=1), jnp.concatenate([-inner_sin, inner_cos], axis=1)], axis=0
+    )
+    stage_last = jnp.concatenate([outer_cos.T, -outer_sin.T], axis=1)
+    return (stage_one, turn_cos, turn_sin, forward_two, inverse_two, stage_last)
+
+
+def conv_kernel(scale, block, fwd_ref, back_ref, one_ref, tc_ref, ts_ref, two_ref, inv_ref, last_ref, out_ref):
+    first = tc_ref.shape[0]
+    second = tc_ref.shape[1]
+
+    def dot(left, right):
+        return jnp.dot(left, right, preferred_element_type=F32)
+
+    def spectrum(signal):
+        outer = dot(one_ref[...], signal)
+        real, imag = outer[:first], outer[first:]
+        turn_c, turn_s = tc_ref[...], ts_ref[...]
+        turned = jnp.concatenate([real * turn_c + imag * turn_s, imag * turn_c - real * turn_s], axis=1)
+        spec = dot(turned.astype(BF16), two_ref[...])
+        return spec[:, :second], spec[:, second:]
+
+    def inverse(real, imag):
+        inner = dot(jnp.concatenate([real, imag], axis=1).astype(BF16), inv_ref[...])
+        inner_re, inner_im = inner[:, :second], inner[:, second:]
+        turn_c, turn_s = tc_ref[...] * scale, ts_ref[...] * scale
+        turned = jnp.concatenate([inner_re * turn_c - inner_im * turn_s, inner_im * turn_c + inner_re * turn_s], axis=0)
+        return dot(last_ref[...], turned.astype(BF16))
+
+    def one_channel(c, carry):
+        g_re, g_im = spectrum(fwd_ref[0, c])
+        t_re, t_im = spectrum(fwd_ref[1, c])
+        out_ref[0, c] = inverse(t_re * g_re - t_im * g_im, t_re * g_im + t_im * g_re).astype(out_ref.dtype)
+        b_re, b_im = spectrum(back_ref[0, c])
+        out_ref[1, c] = inverse(b_re * t_re + b_im * t_im, b_im * t_re - b_re * t_im).astype(out_ref.dtype)
+        out_ref[2, c] = inverse(b_re * g_re + b_im * g_im, b_im * g_re - b_re * g_im).astype(out_ref.dtype)
+        return carry
+
+    lax.fori_loop(0, block, one_channel, 0)
+
+
+def convolve(forward_in, back_part, block=4):
+    _, channels, length = forward_in.shape
+    points = 2 * length
+    second = math.gcd(points, 128)
+    first = points // second
+    half = first // 2
+    tables = kernel_tables(first, second)
+    scale = 1.0 / (math.sqrt(length) * points)
+    fwd = forward_in.reshape(2, channels, half, second)
+    back = back_part.reshape(1, channels, half, second)
+
+    def whole(shape):
+        return pl.BlockSpec(shape, lambda i: (0,) * len(shape))
+
+    out = pl.pallas_call(
+        lambda *refs: conv_kernel(scale, block, *refs),
+        grid=(channels // block,),
+        in_specs=[
+            pl.BlockSpec((2, block, half, second), lambda i: (0, i, 0, 0)),
+            pl.BlockSpec((1, block, half, second), lambda i: (0, i, 0, 0)),
+        ]
+        + [whole(t.shape) for t in tables],
+        out_specs=pl.BlockSpec((3, block, half, second), lambda i: (0, i, 0, 0)),
+        out_shape=jax.ShapeDtypeStruct((3, channels, half, second), BF16),
+        compiler_params=pltpu.CompilerParams(dimension_semantics=("arbitrary",)),
+        name="hyena_conv",
+    )(fwd, back, *tables)
+    return out.reshape(3, channels, length)
+
+
 def body(q_proj, k_proj, v_proj, filter_taps, out_grad):
     query = q_proj.astype(F32)
     key = k_proj.astype(F32)
@@ -104,30 +183,16 @@
     back_in = (cotangent * query).astype(BF16)
 
     forward_in = to_channels([gated, filter_taps])
-    gated_part, taps_part = forward_in[0], forward_in[1]
-    length = gated_part.shape[1]
-    points = 2 * length
-    second = math.gcd(points, 128)
-    first = points // second
-    tables = build_tables(first, second)
-    scale = 1.0 / (math.sqrt(length) * points)
-
-    gated_spec = forward_spectrum(tables, gated_part)
-    taps_spec = forward_spectrum(tables, taps_part)
-    conv_out = inverse_signal(tables, product(taps_spec, gated_spec), scale)
-    conv_back = to_tokens(conv_out.astype(BF16).reshape((1,) + conv_out.shape))[0].astype(F32)
+    back_part = to_channels([back_in])
+    results = convolve(forward_in, back_part)
+    moved = to_tokens(results)
+    conv_back = moved[0].astype(F32)
+    grad_back = moved[1].astype(F32)
     mixed = (query * conv_back).astype(BF16)
     q_grad = (cotangent * conv_back).astype(BF16)
-
-    back_part = to_channels([back_in])[0]
-    back_spec = forward_spectrum(tables, back_part)
-    conv_grad = inverse_signal(tables, product_conj(back_spec, taps_spec), scale)
-    filter_grad = inverse_signal(tables, product_conj(back_spec, gated_spec), scale)
-    second_back = to_tokens(jnp.stack([conv_grad, filter_grad], 0).astype(BF16))
-    grad_back = second_back[0].astype(F32)
     k_grad = (grad_back * value).astype(BF16)
     v_grad = (grad_back * key).astype(BF16)
-    return (mixed, q_grad, k_grad, v_grad, second_back[1])
+    return (mixed, q_grad, k_grad, v_grad, moved[2])
 
 
 def solution(mesh):

time: 225 us -> 183 us (0.81); the launches traced: 222 us -> 182 us
  matrix products: 81 us -> 0 us
  blocking collectives: 0 us -> 46 us
  Pallas kernels: 0 us -> 39.8 us
  waiting for transfers between devices: 62.4 us -> 31.3 us
  starting transfers between devices: 29.5 us -> 17.5 us
  local copies, waits for them, and re-layouts: 35 us -> 30.6 us
  other arithmetic: 12.6 us -> 16.3 us
    dot_general x36 -> x0, matrix products: 81 us -> none  [mm(): jnp.einsum(spec, left.astype(BF16), right.astype(BF16), preferred_element...]
    all_to_all x0 -> x1, blocking collectives: none -> 46 us  [to_tokens(): lax.all_to_all(packed.reshape(devices, count * per_device, rows), AXES, s...]
    pallas_call x0 -> x1, Pallas kernels: none -> 39.8 us  [convolve(): pl.pallas_call(lambda *refs: conv_kernel(scale, block, *refs), grid=(chan...]
    all_to_all x2 -> x0, waiting for transfers between devices: 28.6 us -> none  [to_tokens(): lax.all_to_all(packed.reshape(devices, count * per_device, rows), AXES, s...]
    all_to_all x2 -> x0, starting transfers between devices: 11.5 us -> none  [to_tokens(): lax.all_to_all(packed.reshape(devices, count * per_device, rows), AXES, s...]
    reshape x2 -> x1, local copies, waits for them, and re-layouts: 6.94 us -> 3.92 us  [to_tokens(): packed.reshape(devices, count * per_device, rows)]
    all_to_all x2, waiting for transfers between devices: 33.7 us -> 31.3 us  [to_channels(): lax.all_to_all(packed, AXES, split_axis=0, concat_axis=0, tiled=True)]
    unnamed x30 -> x16, local copies, waits for them, and re-layouts: 19.7 us -> 18 us
  transfers between devices with their start and end apart: 4 -> 2, of which waited for: 4 -> 2; matrix products, arithmetic and copies ran while one was open for 16% -> 10% of each run, Pallas kernels for 0% -> 0%
where the time goes in v1:
time: 183 us; the launch traced here: 182 us
  blocking collectives  46 us (25%)
  Pallas kernels  39.8 us (22%)
  waiting for transfers between devices  31.3 us (17%)
  local copies, waits for them, and re-layouts  30.6 us (17%)
  starting transfers between devices  17.5 us (10%)
  other arithmetic  16.3 us (9%)
    all_to_all x1, blocking collectives, to_tokens(): lax.all_to_all(packed.reshape(devices, count * per_device, rows), AXES, s...  46 us
    pallas_call x1, Pallas kernels, convolve(): pl.pallas_call(lambda *refs: conv_kernel(scale, block, *refs), grid=(chan...  39.8 us
    all_to_all x2, waiting for transfers between devices, to_channels(): lax.all_to_all(packed, AXES, split_axis=0, concat_axis=0, tiled=True)  31.3 us
    unnamed x16, local copies, waits for them, and re-layouts  18 us
    all_to_all x2, starting transfers between devices, to_channels(): lax.all_to_all(packed, AXES, split_axis=0, concat_axis=0, tiled=True)  17.5 us
    all_to_all x2, local copies, waits for them, and re-layouts, to_channels(): lax.all_to_all(packed, AXES, split_axis=0, concat_axis=0, tiled=True)  6.91 us
    reshape x1, local copies, waits for them, and re-layouts, to_tokens(): packed.reshape(devices, count * per_device, rows)  3.92 us
  transfers between devices with their start and end apart: 2, of which 2 were waited for; matrix products, arithmetic and copies ran while one was open for 10% of the time, Pallas kernels for 0%

profile of v1, /device:TPU:0, one launch (start us, length us, event | category | flops | bytes accessed | tf_op | source)
XLA Modules:
  0.0 182.2 jit_solution(17405739533397401262)
XLA Ops:
  0.6 0.0 copy-start.2
  0.6 1.7 copy.38
  2.4 0.0 copy-done.2
  2.4 0.7 copy.43
  3.0 1.2 fusion.1
  4.3 11.7 %all-to-all-start.1 = ((bf16[128,32,128]{2,1,0:T(8,128)(2,1)}), bf16[128,32,128]{2,1,0:T(8,128)(2,1)}, u32[]{:S(2)}, u32[]{:S(2)}) async-start(bf16[128,32,128]{2,1,0:T(8,128)(2,1)} %bitcast.7), calls=%async_computation.1 | async-start | bytes 2097152 | tf_op jit(solution)/shard_map/all_to_all | solution.py:85
  16.0 1.6 copy.39
  17.6 2.3 %copy.40 = bf16[128,4096]{0,1:T(8,128)(2,1)} copy(bf16[128,4096]{1,0:T(8,128)(2,1)} %param.7) | data formatting | bytes 2097152 | tf_op args[2]
  19.9 2.3 %copy.41 = bf16[128,4096]{0,1:T(8,128)(2,1)} copy(bf16[128,4096]{1,0:T(8,128)(2,1)} %param.8) | data formatting | bytes 2097152 | tf_op args[3]
  22.1 0.0 copy-start.1
  22.1 1.6 fusion
  23.7 0.0 copy-done.1
  23.7 1.6 pad_maximum_fusion
  25.3 9.6 %all-to-all-done.1 = bf16[128,32,128]{2,1,0:T(8,128)(2,1)} async-done(((bf16[128,32,128]{2,1,0:T(8,128)(2,1)}), bf16[128,32,128]{2,1,0:T(8,128)(2,1)}, u32[]{:S(2)}, u32[]{:S(2)}) %all-to-all-start.1) | async-done | bytes 1048608 | tf_op jit(solution)/shard_map/all_to_all | solution.py:85
  34.9 5.8 %all-to-all-start = ((bf16[128,64,128]{2,1,0:T(8,128)(2,1)}), bf16[128,64,128]{2,1,0:T(8,128)(2,1)}, u32[]{:S(2)}, u32[]{:S(2)}) async-start(bf16[128,64,128]{2,1,0:T(8,128)(2,1)} %pad_maximum_fusion), calls=%async_computation | async-start | bytes 4194304 | tf_op jit(solution)/shard_map/all_to_all | solution.py:85
  40.7 0.3 fusion.35
  41.0 0.5 fusion.29
  41.5 0.5 fusion.28
  42.0 0.5 cosine_convert_fusion.1
  42.5 0.5 cosine_convert_fusion
  43.0 0.3 sine_convert_fusion.2
  43.3 0.7 pad_maximum_fusion.5.refs_2_
  43.9 0.7 pad_maximum_fusion.6.refs_7_
  44.6 1.2 fusion.32
  45.8 0.7 fusion.7
  46.6 2.6 %copy.52 = bf16[128,32,128]{2,0,1:T(8,128)(2,1)} copy(bf16[128,32,128]{2,1,0:T(8,128)(2,1)} %all-to-all-done.1) | data formatting | bytes 2097152 | tf_op jit(solution)/shard_map/all_to_all | solution.py:85
  49.2 21.7 %all-to-all-done = bf16[128,64,128]{2,1,0:T(8,128)(2,1)} async-done(((bf16[128,64,128]{2,1,0:T(8,128)(2,1)}), bf16[128,64,128]{2,1,0:T(8,128)(2,1)}, u32[]{:S(2)}, u32[]{:S(2)}) %all-to-all-start) | async-done | bytes 2097184 | tf_op jit(solution)/shard_map/all_to_all | solution.py:85
  70.9 4.3 %copy.42 = bf16[128,64,128]{2,0,1:T(8,128)(2,1)} copy(bf16[128,64,128]{2,1,0:T(8,128)(2,1)} %all-to-all-done) | data formatting | bytes 4194304 | tf_op jit(solution)/shard_map/all_to_all | solution.py:85
  75.2 39.8 %hyena_conv.1 = bf16[3,32,128,128]{3,2,1,0:T(8,128)(2,1)} custom-call(bf16[2,32,128,128]{3,2,1,0:T(8,128)(2,1)} %bitcast.34, bf16[1,32,128,128]{3,2,1,0:T(8,128)(2,1)} %bitcast.35, bf16[512,128]{1,0:T(8,128)(2,1)} %pad_maximum_fusion.5.refs_2_, f32[256,128]{1,0:T(8,128)} %get-tuple-element.32.refs_3_, f32[256,128]{1,0:T(8,128)} %get-tuple-element.31.refs_4_, ...), custom_call_target="tpu_custom_call" | custom-call | tf_op jit(solution)/shard_map/hyena_conv/pallas_call | solution.py:161
  115.0 3.9 %copy.45 = bf16[128,96,128]{2,1,0:T(8,128)(2,1)S(1)} copy(bf16[128,96,128]{2,0,1:T(8,128)(2,1)} %bitcast.32) | data formatting | bytes 6291456 | tf_op jit(solution)/shard_map/reshape | solution.py:95
  118.9 46.0 %all_to_all.15 = bf16[128,96,128]{2,1,0:T(8,128)(2,1)S(1)} all-to-all(bf16[128,96,128]{2,1,0:T(8,128)(2,1)S(1)} %copy.45), channel_id=1, replica_groups=mesh['ctx'=16,'ch'=8] {'ctx','ch'}, dimensions={0} | all-to-all | bytes 6291456 | tf_op jit(solution)/shard_map/all_to_all | solution.py:95
  164.9 1.7 fusion.36
  166.7 2.3 %copy.50 = bf16[128,4096]{1,0:T(8,128)(2,1)} copy(bf16[128,4096]{0,1:T(8,128)(2,1)} %bitcast.37) | data formatting | bytes 2097152
  168.9 3.3 %fusion.5 = (bf16[128,4096]{0,1:T(8,128)(2,1)}, bf16[128,4096]{0,1:T(8,128)(2,1)}) fusion(bf16[128,4096]{0,1:T(8,128)(2,1)S(1)} %copy.39, bf16[1,128,128,32]{1,3,0,2:T(8,128)(2,1)} %get-tuple-element.21, bf16[128,4096]{0,1:T(8,128)(2,1)} %copy.40), kind=kLoop, calls=%fused_computation.11 | loop fusion | flops 3670016 | bytes 5242880 | tf_op jit(solution)/shard_map/convert_element_type | solution.py:194
  172.3 2.3 %copy.49 = bf16[128,4096]{1,0:T(8,128)(2,1)} copy(bf16[128,4096]{0,1:T(8,128)(2,1)} %get-tuple-element.23) | data formatting | bytes 2097152
  174.5 2.7 %fusion.3 = (bf16[128,4096]{0,1:T(8,128)(2,1)}, bf16[128,4096]{0,1:T(8,128)(2,1)S(1)}) fusion(bf16[128,4096]{0,1:T(8,128)(2,1)S(1)} %copy.43, bf16[1,128,128,32]{1,3,0,2:T(8,128)(2,1)} %get-tuple-element.22, bf16[128,4096]{0,1:T(8,128)(2,1)S(1)} %copy.38), kind=kLoop, calls=%fused_computation.9 | loop fusion | flops 3670016 | bytes 5242880 | tf_op jit(solution)/shard_map/convert_element_type | solution.py:192
  177.2 0.0 copy-start
  177.2 2.4 %copy.47 = bf16[128,4096]{1,0:T(8,128)(2,1)} copy(bf16[128,4096]{0,1:T(8,128)(2,1)} %get-tuple-element.25) | data formatting | bytes 2097152
  179.5 1.3 copy.46
  180.8 0.0 copy-done
  180.8 1.3 copy.48
Async XLA Ops:
  0.6 1.7 copy-start.2
  4.3 30.6 %all-to-all-start.1 = ((bf16[128,32,128]{2,1,0:T(8,128)(2,1)}), bf16[128,32,128]{2,1,0:T(8,128)(2,1)}, u32[]{:S(2)}, u32[]{:S(2)}) async-start(bf16[128,32,128]{2,1,0:T(8,128)(2,1)} %bitcast.7), calls=%async_computation.1 | async-start | bytes 2097152 | tf_op jit(solution)/shard_map/all_to_all | solution.py:85
  22.1 1.6 copy-start.1
  34.9 35.9 %all-to-all-start = ((bf16[128,64,128]{2,1,0:T(8,128)(2,1)}), bf16[128,64,128]{2,1,0:T(8,128)(2,1)}, u32[]{:S(2)}, u32[]{:S(2)}) async-start(bf16[128,64,128]{2,1,0:T(8,128)(2,1)} %pad_maximum_fusion), calls=%async_computation | async-start | bytes 4194304 | tf_op jit(solution)/shard_map/all_to_all | solution.py:85
  177.2 3.7 %copy-start = (bf16[128,4096]{0,1:T(8,128)(2,1)S(1)}, bf16[128,4096]{0,1:T(8,128)(2,1)}, u32[]{:S(2)}) copy-start(bf16[128,4096]{0,1:T(8,128)(2,1)} %get-tuple-element.24) | copy-start | bytes 3145732

commit v2 on v1

--- a/solution.py
+++ b/solution.py
@@ -174,7 +174,7 @@
     return out.reshape(3, channels, length)
 
 
-def body(q_proj, k_proj, v_proj, filter_taps, out_grad):
+def body(q_proj, k_proj, v_proj, filter_taps, out_grad, chunks=2):
     query = q_proj.astype(F32)
     key = k_proj.astype(F32)
     value = v_proj.astype(F32)
@@ -182,10 +182,12 @@
     gated = (key * value).astype(BF16)
     back_in = (cotangent * query).astype(BF16)
 
-    forward_in = to_channels([gated, filter_taps])
-    back_part = to_channels([back_in])
-    results = convolve(forward_in, back_part)
-    moved = to_tokens(results)
+    width = gated.shape[1] // chunks
+    inputs = [
+        to_channels([a[:, h * width:(h + 1) * width] for a in (gated, filter_taps, back_in)]) for h in range(chunks)
+    ]
+    pieces = [to_tokens(convolve(part[:2], part[2:])) for part in inputs]
+    moved = jnp.concatenate(pieces, axis=2)
     conv_back = moved[0].astype(F32)
     grad_back = moved[1].astype(F32)
     mixed = (query * conv_back).astype(BF16)

time: 183 us -> 179 us (0.978)
  blocking collectives: 46 us -> 0 us
  starting transfers between devices: 17.5 us -> 36.2 us
  waiting for transfers between devices: 31.3 us -> 44.3 us
  local copies, waits for them, and re-layouts: 30.6 us -> 37.4 us
  Pallas kernels: 39.8 us -> 41.8 us
    all_to_all x1 -> x0, blocking collectives: 46 us -> none  [to_tokens(): lax.all_to_all(packed.reshape(devices, count * per_device, rows), AXES, s...]
    all_to_all x0 -> x2, waiting for transfers between devices: none -> 22.9 us  [to_tokens(): lax.all_to_all(packed.reshape(devices, count * per_device, rows), AXES, s...]
    all_to_all x0 -> x2, starting transfers between devices: none -> 20.4 us  [to_tokens(): lax.all_to_all(packed.reshape(devices, count * per_device, rows), AXES, s...]
    all_to_all x2, waiting for transfers between devices: 31.3 us -> 21.3 us  [to_channels(): lax.all_to_all(packed, AXES, split_axis=0, concat_axis=0, tiled=True)]
    all_to_all x2, local copies, waits for them, and re-layouts: 6.91 us -> 2.22 us  [to_channels(): lax.all_to_all(packed, AXES, split_axis=0, concat_axis=0, tiled=True)]
    slice x1 -> x7, local copies, waits for them, and re-layouts: 1.74 us -> 5.94 us  [the longest x4 3.74 us: body(): pieces = [to_tokens(convolve(part[:2], part[2:])) for part in inputs]]
    transpose x0 -> x2, local copies, waits for them, and re-layouts: none -> 3.51 us  [to_tokens(): moved.reshape(devices, count, per_device, rows).transpose(1, 3, 0, 2)]
    concatenate x1 -> x2, other arithmetic: 1.58 us -> 4.92 us  [to_channels(): jnp.concatenate([a.T.reshape(devices, per_device, rows) for a in arrays],...]
  transfers between devices with their start and end apart: 2 -> 4, of which waited for: 2 -> 2; matrix products, arithmetic and copies ran while one was open for 10% -> 14% of each run, Pallas kernels for 0% -> 23%
where the time goes in v2:
time: 179 us
  waiting for transfers between devices  44.3 us (25%)
  Pallas kernels  41.8 us (23%)
  local copies, waits for them, and re-layouts  37.4 us (21%)
  starting transfers between devices  36.2 us (20%)
  other arithmetic  18 us (10%)
    pallas_call x2, Pallas kernels, convolve(): pl.pallas_call(lambda *refs: conv_kernel(scale, block, *refs), grid=(chan...  41.8 us
    all_to_all x2, waiting for transfers between devices, to_tokens(): lax.all_to_all(packed.reshape(devices, count * per_device, rows), AXES, s...  22.9 us
    all_to_all x2, waiting for transfers between devices, to_channels(): lax.all_to_all(packed, AXES, split_axis=0, concat_axis=0, tiled=True)  21.3 us
    all_to_all x2, starting transfers between devices, to_tokens(): lax.all_to_all(packed.reshape(devices, count * per_device, rows), AXES, s...  20.4 us
    unnamed x39, local copies, waits for them, and re-layouts  18.5 us
    all_to_all x2, starting transfers between devices, to_channels(): lax.all_to_all(packed, AXES, split_axis=0, concat_axis=0, tiled=True)  15.8 us
    reshape x2, local copies, waits for them, and re-layouts, to_tokens(): packed.reshape(devices, count * per_device, rows)  7.19 us
    convert_element_type x1, other arithmetic, body(): v_grad = (grad_back * key).astype(BF16)  6.58 us
  transfers between devices with their start and end apart: 4, of which 2 were waited for; matrix products, arithmetic and copies ran while one was open for 14% of the time, Pallas kernels for 23%

profile of v2, /device:TPU:0, one launch (start us, length us, event | category | flops | bytes accessed | tf_op | source)
XLA Modules:
  0.0 178.5 jit_solution(2594193013627059388)
XLA Ops:
  0.6 1.7 copy.31
  2.4 0.7 copy.32
  3.0 2.6 %copy.33 = bf16[128,4096]{0,1:T(8,128)(2,1)} copy(bf16[128,4096]{1,0:T(8,128)(2,1)} %param.7) | data formatting | bytes 2097152 | tf_op args[2]
  5.7 1.6 copy.35
  7.6 0.7 copy-done.4
  8.3 1.0 fusion.43
  9.3 0.6 copy-done.2
  10.2 1.1 fusion.41
  11.2 0.5 copy-done.13
  12.2 0.7 copy-done.11
  12.8 2.3 %pad_maximum_fusion = bf16[128,48,128]{2,1,0:T(8,128)(2,1)} fusion(bf16[128,16,128]{2,1,0:T(8,128)(2,1)S(1)} %bitcast.68, bf16[128,16,128]{2,1,0:T(8,128)(2,1)S(1)} %bitcast.65, bf16[128,16,128]{2,1,0:T(8,128)(2,1)} %bitcast.69), kind=kLoop, calls=%fused_computation.16 | loop fusion | flops 4718592 | bytes 3145728 | tf_op jit(solution)/shard_map/concatenate | solution.py:84
  15.1 11.2 %all-to-all-start = ((bf16[128,48,128]{2,1,0:T(8,128)(2,1)}), bf16[128,48,128]{2,1,0:T(8,128)(2,1)S(1)}, u32[]{:S(2)}, u32[]{:S(2)}) async-start(bf16[128,48,128]{2,1,0:T(8,128)(2,1)} %pad_maximum_fusion), calls=%async_computation | async-start | bytes 3145728 | tf_op jit(solution)/shard_map/all_to_all | solution.py:85
  26.3 1.0 copy.49
  27.3 2.6 %pad_maximum_fusion.1 = bf16[128,48,128]{2,1,0:T(8,128)(2,1)} fusion(bf16[128,16,128]{2,1,0:T(8,128)(2,1)} %bitcast.66, bf16[128,16,128]{2,1,0:T(8,128)(2,1)} %bitcast.64, bf16[128,16,128]{2,1,0:T(8,128)(2,1)} %bitcast.67), kind=kLoop, calls=%fused_computation.17 | loop fusion | flops 4718592 | bytes 3145728 | tf_op jit(solution)/shard_map/concatenate | solution.py:84
  29.9 21.3 %all-to-all-done = bf16[128,48,128]{2,1,0:T(8,128)(2,1)S(1)} async-done(((bf16[128,48,128]{2,1,0:T(8,128)(2,1)}), bf16[128,48,128]{2,1,0:T(8,128)(2,1)S(1)}, u32[]{:S(2)}, u32[]{:S(2)}) %all-to-all-start) | async-done | bytes 1572896 | tf_op jit(solution)/shard_map/all_to_all | solution.py:85
  51.2 1.1 copy-done.6
  52.4 4.6 %all-to-all-start.2 = ((bf16[128,48,128]{2,1,0:T(8,128)(2,1)}), bf16[128,48,128]{2,1,0:T(8,128)(2,1)S(1)}, u32[]{:S(2)}, u32[]{:S(2)}) async-start(bf16[128,48,128]{2,1,0:T(8,128)(2,1)} %pad_maximum_fusion.1), calls=%async_computation.2 | async-start | bytes 3145728 | tf_op jit(solution)/shard_map/all_to_all | solution.py:85
  57.3 0.5 fusion.34
  57.8 0.5 fusion.33
  58.3 0.5 cosine_convert_fusion.1
  58.8 0.5 cosine_convert_fusion
  59.3 0.3 sine_convert_fusion.2
  59.6 0.7 pad_maximum_fusion.7.refs_2_
  60.3 0.7 pad_maximum_fusion.8.refs_7_
  61.0 1.2 fusion.37
  62.2 0.7 fusion.12
  62.9 1.8 %copy.36 = bf16[128,48,128]{2,0,1:T(8,128)(2,1)S(1)} copy(bf16[128,48,128]{2,1,0:T(8,128)(2,1)} %copy-done.6) | data formatting | bytes 3145728 | tf_op jit(solution)/shard_map/all_to_all | solution.py:85
  64.8 0.8 slice.59.refs_1_
  65.6 1.0 slice.58.refs_0_
  66.6 20.9 %hyena_conv.2 = bf16[3,16,128,128]{3,2,1,0:T(8,128)(2,1)} custom-call(bf16[2,16,128,128]{3,2,1,0:T(8,128)(2,1)} %slice.58.refs_0_, bf16[1,16,128,128]{3,2,1,0:T(8,128)(2,1)} %slice.59.refs_1_, bf16[512,128]{1,0:T(8,128)(2,1)} %pad_maximum_fusion.7.refs_2_, f32[256,128]{1,0:T(8,128)} %get-tuple-element.30.refs_3_, f32[256,128]{1,0:T(8,128)} %get-tuple-element.29.refs_4_, ...), custom_call_target="tpu_custom_call" | custom-call | tf_op jit(solution)/shard_map/hyena_conv/pallas_call | solution.py:161
  87.5 3.6 %copy.37 = bf16[128,48,128]{2,1,0:T(8,128)(2,1)} copy(bf16[128,48,128]{2,0,1:T(8,128)(2,1)} %bitcast.63) | data formatting | bytes 3145728 | tf_op jit(solution)/shard_map/reshape | solution.py:95
  91.1 10.4 %all-to-all-start.1 = ((bf16[128,48,128]{2,1,0:T(8,128)(2,1)}), bf16[128,48,128]{2,1,0:T(8,128)(2,1)}, u32[]{:S(2)}, u32[]{:S(2)}) async-start(bf16[128,48,128]{2,1,0:T(8,128)(2,1)} %copy.37), calls=%async_computation.1 | async-start | bytes 3145728 | tf_op jit(solution)/shard_map/all_to_all | solution.py:95
  101.5 0.4 copy.40
  101.9 0.8 slice.63.refs_1_
  102.8 1.0 slice.62.refs_0_
  103.8 20.9 %hyena_conv.3 = bf16[3,16,128,128]{3,2,1,0:T(8,128)(2,1)} custom-call(bf16[2,16,128,128]{3,2,1,0:T(8,128)(2,1)} %slice.62.refs_0_, bf16[1,16,128,128]{3,2,1,0:T(8,128)(2,1)} %slice.63.refs_1_, bf16[512,128]{1,0:T(8,128)(2,1)} %pad_maximum_fusion.7.refs_2_, f32[256,128]{1,0:T(8,128)} %get-tuple-element.30.refs_3_, f32[256,128]{1,0:T(8,128)} %get-tuple-element.29.refs_4_, ...), custom_call_target="tpu_custom_call" | custom-call | tf_op jit(solution)/shard_map/hyena_conv/pallas_call | solution.py:161
  124.7 3.6 %copy.41 = bf16[128,48,128]{2,1,0:T(8,128)(2,1)} copy(bf16[128,48,128]{2,0,1:T(8,128)(2,1)} %bitcast.62) | data formatting | bytes 3145728 | tf_op jit(solution)/shard_map/reshape | solution.py:95
  128.4 10.0 %all-to-all-start.3 = ((bf16[128,48,128]{2,1,0:T(8,128)(2,1)}), bf16[128,48,128]{2,1,0:T(8,128)(2,1)}, u32[]{:S(2)}, u32[]{:S(2)}) async-start(bf16[128,48,128]{2,1,0:T(8,128)(2,1)} %copy.41), calls=%async_computation.3 | async-start | bytes 3145728 | tf_op jit(solution)/shard_map/all_to_all | solution.py:95
  138.4 1.7 copy.38
  140.0 22.9 %all-to-all-done.3 = bf16[128,48,128]{2,1,0:T(8,128)(2,1)} async-done(((bf16[128,48,128]{2,1,0:T(8,128)(2,1)}), bf16[128,48,128]{2,1,0:T(8,128)(2,1)}, u32[]{:S(2)}, u32[]{:S(2)}) %all-to-all-start.3) | async-done | bytes 1572896 | tf_op jit(solution)/shard_map/all_to_all | solution.py:95
  163.0 1.8 %copy.42 = bf16[3,128,128,16]{1,3,2,0:T(8,128)(2,1)S(1)} copy(bf16[3,128,128,16]{1,3,0,2:T(8,128)(2,1)} %bitcast.26) | data formatting | bytes 3145728 | tf_op jit(solution)/shard_map/transpose | solution.py:96
  165.0 0.3 copy-done.5
  165.3 6.6 %fusion.5 = (bf16[128,4096]{0,1:T(8,128)(2,1)}, bf16[128,4096]{0,1:T(8,128)(2,1)}, bf16[128,4096]{0,1:T(8,128)(2,1)}, bf16[128,4096]{0,1:T(8,128)(2,1)}) fusion(bf16[128,4096]{0,1:T(8,128)(2,1)S(1)} %copy-done.1, bf16[3,128,2048]{1,2,0:T(8,128)(2,1)S(1)} %bitcast.56, bf16[3,128,2048]{1,2,0:T(8,128)(2,1)S(1)} %bitcast.54, bf16[128,4096]{0,1:T(8,128)(2,1)S(1)} %copy-done.5, ...), kind=kLoop, calls=%fused_computation.15 | loop fusion | flops 16777216 | bytes 11534336 | tf_op jit(solution)/shard_map/convert_element_type | solution.py:196
  172.0 1.3 copy.47
  173.3 1.3 copy.46
  174.6 1.3 copy.44
  175.9 1.3 copy.43
  177.2 1.3 copy.45
  (30 shorter events, 1.5 us)
Async XLA Ops:
  0.6 1.7 copy-start.12
  3.0 6.3 %copy-start = (bf16[128,4096]{0,1:T(8,128)(2,1)}, bf16[128,4096]{0,1:T(8,128)(2,1)S(1)}, u32[]{:S(2)}) copy-start(bf16[128,4096]{0,1:T(8,128)(2,1)S(1)} %copy.32) | copy-start | bytes 3145732
  7.3 1.0 copy-start.4
  8.3 1.6 copy-start.2
  10.2 1.6 copy-start.13
  11.8 1.0 copy-start.11
  15.1 36.1 %all-to-all-start = ((bf16[128,48,128]{2,1,0:T(8,128)(2,1)}), bf16[128,48,128]{2,1,0:T(8,128)(2,1)S(1)}, u32[]{:S(2)}, u32[]{:S(2)}) async-start(bf16[128,48,128]{2,1,0:T(8,128)(2,1)} %pad_maximum_fusion), calls=%async_computation | async-start | bytes 3145728 | tf_op jit(solution)/shard_map/all_to_all | solution.py:85
  51.2 1.1 copy-start.6
  52.4 38.7 %all-to-all-start.2 = ((bf16[128,48,128]{2,1,0:T(8,128)(2,1)}), bf16[128,48,128]{2,1,0:T(8,128)(2,1)S(1)}, u32[]{:S(2)}, u32[]{:S(2)}) async-start(bf16[128,48,128]{2,1,0:T(8,128)(2,1)} %pad_maximum_fusion.1), calls=%async_computation.2 | async-start | bytes 3145728 | tf_op jit(solution)/shard_map/all_to_all | solution.py:85
  91.1 37.2 %all-to-all-start.1 = ((bf16[128,48,128]{2,1,0:T(8,128)(2,1)}), bf16[128,48,128]{2,1,0:T(8,128)(2,1)}, u32[]{:S(2)}, u32[]{:S(2)}) async-start(bf16[128,48,128]{2,1,0:T(8,128)(2,1)} %copy.37), calls=%async_computation.1 | async-start | bytes 3145728 | tf_op jit(solution)/shard_map/all_to_all | solution.py:95
  128.4 34.6 %all-to-all-start.3 = ((bf16[128,48,128]{2,1,0:T(8,128)(2,1)}), bf16[128,48,128]{2,1,0:T(8,128)(2,1)}, u32[]{:S(2)}, u32[]{:S(2)}) async-start(bf16[128,48,128]{2,1,0:T(8,128)(2,1)} %copy.41), calls=%async_computation.3 | async-start | bytes 3145728 | tf_op jit(solution)/shard_map/all_to_all | solution.py:95
  163.0 1.8 %copy-start.1 = (bf16[128,4096]{0,1:T(8,128)(2,1)S(1)}, bf16[128,4096]{0,1:T(8,128)(2,1)}, u32[]{:S(2)}) copy-start(bf16[128,4096]{0,1:T(8,128)(2,1)} %copy-done) | copy-start | bytes 3145732
  163.0 2.0 %copy-start.3 = (bf16[128,4096]{0,1:T(8,128)(2,1)S(1)}, bf16[128,4096]{0,1:T(8,128)(2,1)}, u32[]{:S(2)}) copy-start(bf16[128,4096]{0,1:T(8,128)(2,1)} %copy.33) | copy-start | bytes 3145732
  163.0 2.3 %copy-start.5 = (bf16[128,4096]{0,1:T(8,128)(2,1)S(1)}, bf16[128,4096]{0,1:T(8,128)(2,1)}, u32[]{:S(2)}) copy-start(bf16[128,4096]{0,1:T(8,128)(2,1)} %copy-done.4) | copy-start | bytes 3145732
  171.9 1.3 copy-start.10
  173.3 1.3 copy-start.9
  174.6 1.3 copy-start.8
  175.9 1.3 copy-start.7

commit v3 on v2

--- a/solution.py
+++ b/solution.py
@@ -97,61 +97,88 @@
     return moved.reshape(count, rows, devices * per_device)
 
 
-def kernel_tables(first, second):
+def kernel_tables(first, second, rows):
     outer_cos, outer_sin, turn_cos, turn_sin, inner_cos, inner_sin = build_tables(first, second)
-    stage_one = jnp.concatenate([outer_cos, -outer_sin], axis=0)
+    stage_one = jnp.concatenate([outer_cos[:rows], -outer_sin[:rows]], axis=0)
     forward_two = jnp.concatenate(
         [jnp.concatenate([inner_cos, -inner_sin], axis=1), jnp.concatenate([inner_sin, inner_cos], axis=1)], axis=0
     )
     inverse_two = jnp.concatenate(
         [jnp.concatenate([inner_cos, inner_sin], axis=1), jnp.concatenate([-inner_sin, inner_cos], axis=1)], axis=0
     )
-    stage_last = jnp.concatenate([outer_cos.T, -outer_sin.T], axis=1)
-    return (stage_one, turn_cos, turn_sin, forward_two, inverse_two, stage_last)
-
-
-def conv_kernel(scale, block, fwd_ref, back_ref, one_ref, tc_ref, ts_ref, two_ref, inv_ref, last_ref, out_ref):
+    index = jnp.arange(rows)
+    weight = jnp.where((index == 0) | (index == first // 2), 1.0, jnp.where(index < first // 2, 2.0, 0.0))
+    weight = weight.astype(F32)[None, :]
+    stage_last = jnp.concatenate(
+        [outer_cos[:rows].T.astype(F32) * weight, -outer_sin[:rows].T.astype(F32) * weight], axis=1
+    )
+    return (stage_one, turn_cos[:rows], turn_sin[:rows], forward_two, inverse_two, stage_last)
+
+
+def conv_kernel(block, fwd_ref, back_ref, one_ref, tc_ref, ts_ref, two_ref, inv_ref, last_ref, out_ref, turned_ref, spec_ref):
     first = tc_ref.shape[0]
     second = tc_ref.shape[1]
 
     def dot(left, right):
         return jnp.dot(left, right, preferred_element_type=F32)
 
-    def spectrum(signal):
-        outer = dot(one_ref[...], signal)
-        real, imag = outer[:first], outer[first:]
+    def rows_of(signal, c):
+        return pl.ds(pl.multiple_of((signal * block + c) * first, first), first)
+
+    def stage_one(c, carry):
+        for signal, source in enumerate((fwd_ref.at[0], fwd_ref.at[1], back_ref.at[0])):
+            outer = dot(one_ref[...], source[c])
+            real, imag = outer[:first], outer[first:]
+            turn_c, turn_s = tc_ref[...], ts_ref[...]
+            turned = jnp.concatenate([real * turn_c + imag * turn_s, imag * turn_c - real * turn_s], axis=1)
+            turned_ref[rows_of(signal, c), :] = turned.astype(BF16)
+        return carry
+
+    lax.fori_loop(0, block, stage_one, 0)
+    spec_ref[...] = dot(turned_ref[...], two_ref[...])
+
+    def products(c, carry):
+        g = spec_ref[rows_of(0, c), :]
+        t = spec_ref[rows_of(1, c), :]
+        b = spec_ref[rows_of(2, c), :]
+        g_re, g_im = g[:, :second], g[:, second:]
+        t_re, t_im = t[:, :second], t[:, second:]
+        b_re, b_im = b[:, :second], b[:, second:]
+        pairs = (
+            (t_re * g_re - t_im * g_im, t_re * g_im + t_im * g_re),
+            (b_re * t_re + b_im * t_im, b_im * t_re - b_re * t_im),
+            (b_re * g_re + b_im * g_im, b_im * g_re - b_re * g_im),
+        )
+        for j, (real, imag) in enumerate(pairs):
+            turned_ref[rows_of(j, c), :] = jnp.concatenate([real, imag], axis=1).astype(BF16)
+        return carry
+
+    lax.fori_loop(0, block, products, 0)
+    spec_ref[...] = dot(turned_ref[...], inv_ref[...])
+
+    def stage_last(c, carry):
         turn_c, turn_s = tc_ref[...], ts_ref[...]
-        turned = jnp.concatenate([real * turn_c + imag * turn_s, imag * turn_c - real * turn_s], axis=1)
-        spec = dot(turned.astype(BF16), two_ref[...])
-        return spec[:, :second], spec[:, second:]
-
-    def inverse(real, imag):
-        inner = dot(jnp.concatenate([real, imag], axis=1).astype(BF16), inv_ref[...])
-        inner_re, inner_im = inner[:, :second], inner[:, second:]
-        turn_c, turn_s = tc_ref[...] * scale, ts_ref[...] * scale
-        turned = jnp.concatenate([inner_re * turn_c - inner_im * turn_s, inner_im * turn_c + inner_re * turn_s], axis=0)
-        return dot(last_ref[...], turned.astype(BF16))
-
-    def one_channel(c, carry):
-        g_re, g_im = spectrum(fwd_ref[0, c])
-        t_re, t_im = spectrum(fwd_ref[1, c])
-        out_ref[0, c] = inverse(t_re * g_re - t_im * g_im, t_re * g_im + t_im * g_re).astype(out_ref.dtype)
-        b_re, b_im = spectrum(back_ref[0, c])
-        out_ref[1, c] = inverse(b_re * t_re + b_im * t_im, b_im * t_re - b_re * t_im).astype(out_ref.dtype)
-        out_ref[2, c] = inverse(b_re * g_re + b_im * g_im, b_im * g_re - b_re * g_im).astype(out_ref.dtype)
+        for j in range(3):
+            inner = spec_ref[rows_of(j, c), :]
+            inner_re, inner_im = inner[:, :second], inner[:, second:]
+            turned = jnp.concatenate(
+                [inner_re * turn_c - inner_im * turn_s, inner_im * turn_c + inner_re * turn_s], axis=0
+            )
+            out_ref[j, c] = dot(last_ref[...], turned.astype(BF16)).astype(out_ref.dtype)
         return carry
 
-    lax.fori_loop(0, block, one_channel, 0)
-
-
-def convolve(forward_in, back_part, block=4):
+    lax.fori_loop(0, block, stage_last, 0)
+
+
+def convolve(forward_in, back_part, block=8, rows=144):
     _, channels, length = forward_in.shape
     points = 2 * length
     second = math.gcd(points, 128)
     first = points // second
     half = first // 2
-    tables = kernel_tables(first, second)
     scale = 1.0 / (math.sqrt(length) * points)
+    stage_one, turn_c, turn_s, forward_two, inverse_two, stage_last = kernel_tables(first, second, rows)
+    tables = (stage_one, turn_c, turn_s, forward_two, inverse_two, (stage_last.astype(F32) * scale).astype(BF16))
     fwd = forward_in.reshape(2, channels, half, second)
     back = back_part.reshape(1, channels, half, second)
 
@@ -159,7 +186,7 @@
         return pl.BlockSpec(shape, lambda i: (0,) * len(shape))
 
     out = pl.pallas_call(
-        lambda *refs: conv_kernel(scale, block, *refs),
+        lambda *refs: conv_kernel(block, *refs),
         grid=(channels // block,),
         in_specs=[
             pl.BlockSpec((2, block, half, second), lambda i: (0, i, 0, 0)),
@@ -168,6 +195,7 @@
         + [whole(t.shape) for t in tables],
         out_specs=pl.BlockSpec((3, block, half, second), lambda i: (0, i, 0, 0)),
         out_shape=jax.ShapeDtypeStruct((3, channels, half, second), BF16),
+        scratch_shapes=[pltpu.VMEM((3 * block * rows, 2 * second), BF16), pltpu.VMEM((3 * block * rows, 2 * second), F32)],
         compiler_params=pltpu.CompilerParams(dimension_semantics=("arbitrary",)),
         name="hyena_conv",
     )(fwd, back, *tables)

time: 179 us -> 167 us (0.933)
  Pallas kernels: 41.8 us -> 29.4 us
  starting transfers between devices: 36.2 us -> 32.4 us
  waiting for transfers between devices: 44.3 us -> 48.1 us
  other arithmetic: 18 us -> 15.3 us
  local copies, waits for them, and re-layouts: 37.4 us -> 40 us
    pallas_call x2, Pallas kernels: 41.8 us -> 29.4 us  [convolve(): pl.pallas_call(lambda *refs: conv_kernel(block, *refs), grid=(channels //...]
    all_to_all x2, waiting for transfers between devices: 22.9 us -> 26.8 us  [to_tokens(): lax.all_to_all(packed.reshape(devices, count * per_device, rows), AXES, s...]
    all_to_all x2, starting transfers between devices: 20.4 us -> 16.6 us  [to_tokens(): lax.all_to_all(packed.reshape(devices, count * per_device, rows), AXES, s...]
  transfers between devices with their start and end apart: 4 -> 4, of which waited for: 2 -> 3; matrix products, arithmetic and copies ran while one was open for 14% -> 15% of each run, Pallas kernels for 23% -> 18%
where the time goes in v3:
time: 167 us; the launch traced here: 166 us
  waiting for transfers between devices  48.1 us (29%)
  local copies, waits for them, and re-layouts  40 us (24%)
  starting transfers between devices  32.4 us (19%)
  Pallas kernels  29.4 us (18%)
  other arithmetic  15.3 us (9%)
    pallas_call x2, Pallas kernels, convolve(): pl.pallas_call(lambda *refs: conv_kernel(block, *refs), grid=(channels //...  29.4 us
    all_to_all x2, waiting for transfers between devices, to_tokens(): lax.all_to_all(packed.reshape(devices, count * per_device, rows), AXES, s...  26.8 us
    all_to_all x2, waiting for transfers between devices, to_channels(): lax.all_to_all(packed, AXES, split_axis=0, concat_axis=0, tiled=True)  21.3 us
    unnamed x39, local copies, waits for them, and re-layouts  18.5 us
    all_to_all x2, starting transfers between devices, to_tokens(): lax.all_to_all(packed.reshape(devices, count * per_device, rows), AXES, s...  16.6 us
    all_to_all x2, starting transfers between devices, to_channels(): lax.all_to_all(packed, AXES, split_axis=0, concat_axis=0, tiled=True)  15.8 us
    reshape x2, local copies, waits for them, and re-layouts, to_tokens(): packed.reshape(devices, count * per_device, rows)  7.19 us
    convert_element_type x1, other arithmetic, body(): v_grad = (grad_back * key).astype(BF16)  6.58 us
  transfers between devices with their start and end apart: 4, of which 3 were waited for; matrix products, arithmetic and copies ran while one was open for 15% of the time, Pallas kernels for 18%

profile of v3, /device:TPU:0, one launch (start us, length us, event | category | flops | bytes accessed | tf_op | source)
XLA Modules:
  0.0 166.0 jit_solution(4476113280404170312)
XLA Ops:
  0.6 1.7 %copy.43 = bf16[128,4096]{0,1:T(8,128)(2,1)S(1)} copy(bf16[128,4096]{1,0:T(8,128)(2,1)} %param.5) | data formatting | bytes 2097152 | tf_op args[0]
  2.4 0.7 copy.44
  3.0 2.6 %copy.45 = bf16[128,4096]{0,1:T(8,128)(2,1)} copy(bf16[128,4096]{1,0:T(8,128)(2,1)} %param.7) | data formatting | bytes 2097152 | tf_op args[2]
  5.7 1.6 copy.47
  7.6 0.7 copy-done.4
  8.3 1.0 fusion.38
  9.3 0.6 copy-done.2
  10.2 1.0 fusion.36
  11.2 0.5 copy-done.13
  12.2 0.7 copy-done.11
  12.8 2.3 %pad_maximum_fusion = bf16[128,48,128]{2,1,0:T(8,128)(2,1)} fusion(bf16[128,16,128]{2,1,0:T(8,128)(2,1)S(1)} %bitcast.72, bf16[128,16,128]{2,1,0:T(8,128)(2,1)S(1)} %bitcast.69, bf16[128,16,128]{2,1,0:T(8,128)(2,1)} %bitcast.73), kind=kLoop, calls=%fused_computation.16 | loop fusion | flops 4718592 | bytes 3145728 | tf_op jit(solution)/shard_map/concatenate | solution.py:84
  15.1 11.2 %all-to-all-start = ((bf16[128,48,128]{2,1,0:T(8,128)(2,1)}), bf16[128,48,128]{2,1,0:T(8,128)(2,1)S(1)}, u32[]{:S(2)}, u32[]{:S(2)}) async-start(bf16[128,48,128]{2,1,0:T(8,128)(2,1)} %pad_maximum_fusion), calls=%async_computation | async-start | bytes 3145728 | tf_op jit(solution)/shard_map/all_to_all | solution.py:85
  26.3 1.0 copy.67
  27.3 2.6 %pad_maximum_fusion.1 = bf16[128,48,128]{2,1,0:T(8,128)(2,1)} fusion(bf16[128,16,128]{2,1,0:T(8,128)(2,1)} %bitcast.70, bf16[128,16,128]{2,1,0:T(8,128)(2,1)} %bitcast.68, bf16[128,16,128]{2,1,0:T(8,128)(2,1)} %bitcast.71), kind=kLoop, calls=%fused_computation.17 | loop fusion | flops 4718592 | bytes 3145728 | tf_op jit(solution)/shard_map/concatenate | solution.py:84
  29.9 21.3 %all-to-all-done = bf16[128,48,128]{2,1,0:T(8,128)(2,1)S(1)} async-done(((bf16[128,48,128]{2,1,0:T(8,128)(2,1)}), bf16[128,48,128]{2,1,0:T(8,128)(2,1)S(1)}, u32[]{:S(2)}, u32[]{:S(2)}) %all-to-all-start) | async-done | bytes 1572896 | tf_op jit(solution)/shard_map/all_to_all | solution.py:85
  51.2 1.1 copy-done.6
  52.4 4.6 %all-to-all-start.2 = ((bf16[128,48,128]{2,1,0:T(8,128)(2,1)}), bf16[128,48,128]{2,1,0:T(8,128)(2,1)S(1)}, u32[]{:S(2)}, u32[]{:S(2)}) async-start(bf16[128,48,128]{2,1,0:T(8,128)(2,1)} %pad_maximum_fusion.1), calls=%async_computation.2 | async-start | bytes 3145728 | tf_op jit(solution)/shard_map/all_to_all | solution.py:85
  57.1 0.5 slice_sine_fusion
  57.6 0.7 copy.51.refs_4_
  58.3 0.7 copy.50.refs_3_
  59.1 0.4 fusion.31
  59.5 0.5 multiply_bitcast_fusion.1
  60.1 0.8 copy.49.refs_2_
  61.4 0.7 fusion.11.refs_7_
  62.2 0.7 fusion.13
  62.9 1.8 %copy.48 = bf16[128,48,128]{2,0,1:T(8,128)(2,1)S(1)} copy(bf16[128,48,128]{2,1,0:T(8,128)(2,1)} %copy-done.6) | data formatting | bytes 3145728 | tf_op jit(solution)/shard_map/all_to_all | solution.py:85
  64.7 0.8 slice.91.refs_1_
  65.6 1.0 slice.90.refs_0_
  66.6 14.7 %hyena_conv.2 = bf16[3,16,128,128]{3,2,1,0:T(8,128)(2,1)} custom-call(bf16[2,16,128,128]{3,2,1,0:T(8,128)(2,1)} %slice.90.refs_0_, bf16[1,16,128,128]{3,2,1,0:T(8,128)(2,1)} %slice.91.refs_1_, bf16[288,128]{1,0:T(8,128)(2,1)} %copy.49.refs_2_, f32[144,128]{1,0:T(8,128)} %copy.50.refs_3_, f32[144,128]{1,0:T(8,128)} %copy.51.refs_4_, ...), custom_call_target="tpu_custom_call" | custom-call | tf_op jit(solution)/shard_map/hyena_conv/pallas_call | solution.py:188
  81.3 3.6 %copy.52 = bf16[128,48,128]{2,1,0:T(8,128)(2,1)} copy(bf16[128,48,128]{2,0,1:T(8,128)(2,1)} %bitcast.65) | data formatting | bytes 3145728 | tf_op jit(solution)/shard_map/reshape | solution.py:95
  84.8 10.4 %all-to-all-start.1 = ((bf16[128,48,128]{2,1,0:T(8,128)(2,1)}), bf16[128,48,128]{2,1,0:T(8,128)(2,1)}, u32[]{:S(2)}, u32[]{:S(2)}) async-start(bf16[128,48,128]{2,1,0:T(8,128)(2,1)} %copy.52), calls=%async_computation.1 | async-start | bytes 3145728 | tf_op jit(solution)/shard_map/all_to_all | solution.py:95
  95.3 0.4 copy.55
  95.7 0.8 slice.99.refs_1_
  96.5 1.0 slice.98.refs_0_
  97.5 14.7 %hyena_conv.3 = bf16[3,16,128,128]{3,2,1,0:T(8,128)(2,1)} custom-call(bf16[2,16,128,128]{3,2,1,0:T(8,128)(2,1)} %slice.98.refs_0_, bf16[1,16,128,128]{3,2,1,0:T(8,128)(2,1)} %slice.99.refs_1_, bf16[288,128]{1,0:T(8,128)(2,1)} %copy.49.refs_2_, f32[144,128]{1,0:T(8,128)} %copy.50.refs_3_, f32[144,128]{1,0:T(8,128)} %copy.51.refs_4_, ...), custom_call_target="tpu_custom_call" | custom-call | tf_op jit(solution)/shard_map/hyena_conv/pallas_call | solution.py:188
  112.2 3.6 %copy.59 = bf16[128,48,128]{2,1,0:T(8,128)(2,1)} copy(bf16[128,48,128]{2,0,1:T(8,128)(2,1)} %bitcast.62) | data formatting | bytes 3145728 | tf_op jit(solution)/shard_map/reshape | solution.py:95
  115.8 3.8 %all-to-all-done.1 = bf16[128,48,128]{2,1,0:T(8,128)(2,1)} async-done(((bf16[128,48,128]{2,1,0:T(8,128)(2,1)}), bf16[128,48,128]{2,1,0:T(8,128)(2,1)}, u32[]{:S(2)}, u32[]{:S(2)}) %all-to-all-start.1) | async-done | bytes 1572896 | tf_op jit(solution)/shard_map/all_to_all | solution.py:95
  119.7 6.2 %all-to-all-start.3 = ((bf16[128,48,128]{2,1,0:T(8,128)(2,1)}), bf16[128,48,128]{2,1,0:T(8,128)(2,1)}, u32[]{:S(2)}, u32[]{:S(2)}) async-start(bf16[128,48,128]{2,1,0:T(8,128)(2,1)} %copy.59), calls=%async_computation.3 | async-start | bytes 3145728 | tf_op jit(solution)/shard_map/all_to_all | solution.py:95
  125.9 1.7 %copy.53 = bf16[3,128,128,16]{1,3,2,0:T(8,128)(2,1)S(1)} copy(bf16[3,128,128,16]{1,3,0,2:T(8,128)(2,1)} %bitcast.14) | data formatting | bytes 3145728 | tf_op jit(solution)/shard_map/transpose | solution.py:96
  127.5 22.9 %all-to-all-done.3 = bf16[128,48,128]{2,1,0:T(8,128)(2,1)} async-done(((bf16[128,48,128]{2,1,0:T(8,128)(2,1)}), bf16[128,48,128]{2,1,0:T(8,128)(2,1)}, u32[]{:S(2)}, u32[]{:S(2)}) %all-to-all-start.3) | async-done | bytes 1572896 | tf_op jit(solution)/shard_map/all_to_all | solution.py:95
  150.5 1.8 %copy.60 = bf16[3,128,128,16]{1,3,2,0:T(8,128)(2,1)S(1)} copy(bf16[3,128,128,16]{1,3,0,2:T(8,128)(2,1)} %bitcast.28) | data formatting | bytes 3145728 | tf_op jit(solution)/shard_map/transpose | solution.py:96
  152.5 0.3 copy-done.5
  152.8 6.6 %fusion.5 = (bf16[128,4096]{0,1:T(8,128)(2,1)}, bf16[128,4096]{0,1:T(8,128)(2,1)}, bf16[128,4096]{0,1:T(8,128)(2,1)}, bf16[128,4096]{0,1:T(8,128)(2,1)}) fusion(bf16[128,4096]{0,1:T(8,128)(2,1)S(1)} %copy-done.1, bf16[3,128,2048]{1,2,0:T(8,128)(2,1)S(1)} %bitcast.60, bf16[3,128,2048]{1,2,0:T(8,128)(2,1)S(1)} %bitcast.58, bf16[128,4096]{0,1:T(8,128)(2,1)S(1)} %copy-done.5, ...), kind=kLoop, calls=%fused_computation.15 | loop fusion | flops 16777216 | bytes 11534336 | tf_op jit(solution)/shard_map/convert_element_type | solution.py:224
  159.5 1.3 copy.65
  160.8 1.3 copy.64
  162.1 1.3 copy.62
  163.4 1.3 copy.61
  164.7 1.3 copy.63
  (34 shorter events, 2.0 us)
Async XLA Ops:
  0.6 1.7 %copy-start.12 = (bf16[128,4096]{1,0:T(8,128)(2,1)S(1)}, bf16[128,4096]{1,0:T(8,128)(2,1)}, u32[]{:S(2)}) copy-start(bf16[128,4096]{1,0:T(8,128)(2,1)} %param.6) | copy-start | bytes 3145732
  3.0 6.3 %copy-start = (bf16[128,4096]{0,1:T(8,128)(2,1)}, bf16[128,4096]{0,1:T(8,128)(2,1)S(1)}, u32[]{:S(2)}) copy-start(bf16[128,4096]{0,1:T(8,128)(2,1)S(1)} %copy.44) | copy-start | bytes 3145732
  7.3 1.0 copy-start.4
  8.3 1.6 copy-start.2
  10.2 1.6 copy-start.13
  11.8 1.0 copy-start.11
  15.1 36.1 %all-to-all-start = ((bf16[128,48,128]{2,1,0:T(8,128)(2,1)}), bf16[128,48,128]{2,1,0:T(8,128)(2,1)S(1)}, u32[]{:S(2)}, u32[]{:S(2)}) async-start(bf16[128,48,128]{2,1,0:T(8,128)(2,1)} %pad_maximum_fusion), calls=%async_computation | async-start | bytes 3145728 | tf_op jit(solution)/shard_map/all_to_all | solution.py:85
  51.2 1.1 copy-start.6
  52.4 32.5 %all-to-all-start.2 = ((bf16[128,48,128]{2,1,0:T(8,128)(2,1)}), bf16[128,48,128]{2,1,0:T(8,128)(2,1)S(1)}, u32[]{:S(2)}, u32[]{:S(2)}) async-start(bf16[128,48,128]{2,1,0:T(8,128)(2,1)} %pad_maximum_fusion.1), calls=%async_computation.2 | async-start | bytes 3145728 | tf_op jit(solution)/shard_map/all_to_all | solution.py:85
  84.8 34.8 %all-to-all-start.1 = ((bf16[128,48,128]{2,1,0:T(8,128)(2,1)}), bf16[128,48,128]{2,1,0:T(8,128)(2,1)}, u32[]{:S(2)}, u32[]{:S(2)}) async-start(bf16[128,48,128]{2,1,0:T(8,128)(2,1)} %copy.52), calls=%async_computation.1 | async-start | bytes 3145728 | tf_op jit(solution)/shard_map/all_to_all | solution.py:95
  119.7 30.8 %all-to-all-start.3 = ((bf16[128,48,128]{2,1,0:T(8,128)(2,1)}), bf16[128,48,128]{2,1,0:T(8,128)(2,1)}, u32[]{:S(2)}, u32[]{:S(2)}) async-start(bf16[128,48,128]{2,1,0:T(8,128)(2,1)} %copy.59), calls=%async_computation.3 | async-start | bytes 3145728 | tf_op jit(solution)/shard_map/all_to_all | solution.py:95
  150.5 1.8 %copy-start.1 = (bf16[128,4096]{0,1:T(8,128)(2,1)S(1)}, bf16[128,4096]{0,1:T(8,128)(2,1)}, u32[]{:S(2)}) copy-start(bf16[128,4096]{0,1:T(8,128)(2,1)} %copy-done) | copy-start | bytes 3145732
  150.5 2.0 %copy-start.3 = (bf16[128,4096]{0,1:T(8,128)(2,1)S(1)}, bf16[128,4096]{0,1:T(8,128)(2,1)}, u32[]{:S(2)}) copy-start(bf16[128,4096]{0,1:T(8,128)(2,1)} %copy.45) | copy-start | bytes 3145732
  150.5 2.3 %copy-start.5 = (bf16[128,4096]{0,1:T(8,128)(2,1)S(1)}, bf16[128,4096]{0,1:T(8,128)(2,1)}, u32[]{:S(2)}) copy-start(bf16[128,4096]{0,1:T(8,128)(2,1)} %copy-done.4) | copy-start | bytes 3145732
  159.4 1.3 copy-start.10
  160.8 1.3 copy-start.9
  162.1 1.3 copy-start.8
  163.4 1.3 copy-start.7

commit v4 on v3

--- a/solution.py
+++ b/solution.py
@@ -115,7 +115,7 @@
     return (stage_one, turn_cos[:rows], turn_sin[:rows], forward_two, inverse_two, stage_last)
 
 
-def conv_kernel(block, fwd_ref, back_ref, one_ref, tc_ref, ts_ref, two_ref, inv_ref, last_ref, out_ref, turned_ref, spec_ref):
+def conv_kernel(block, sig_ref, one_ref, tc_ref, ts_ref, two_ref, inv_ref, last_ref, out_ref, turned_ref, spec_ref):
     first = tc_ref.shape[0]
     second = tc_ref.shape[1]
 
@@ -126,7 +126,8 @@
         return pl.ds(pl.multiple_of((signal * block + c) * first, first), first)
 
     def stage_one(c, carry):
-        for signal, source in enumerate((fwd_ref.at[0], fwd_ref.at[1], back_ref.at[0])):
+        for signal in range(3):
+            source = sig_ref.at[signal]
             outer = dot(one_ref[...], source[c])
             real, imag = outer[:first], outer[first:]
             turn_c, turn_s = tc_ref[...], ts_ref[...]
@@ -170,17 +171,18 @@
     lax.fori_loop(0, block, stage_last, 0)
 
 
-def convolve(forward_in, back_part, block=8, rows=144):
-    _, channels, length = forward_in.shape
+def convolve(signals, block=8, rows=None):
+    _, channels, length = signals.shape
     points = 2 * length
     second = math.gcd(points, 128)
     first = points // second
     half = first // 2
     scale = 1.0 / (math.sqrt(length) * points)
+    if rows is None:
+        rows = min(first, -(-(half + 1) // 16) * 16)
     stage_one, turn_c, turn_s, forward_two, inverse_two, stage_last = kernel_tables(first, second, rows)
     tables = (stage_one, turn_c, turn_s, forward_two, inverse_two, (stage_last.astype(F32) * scale).astype(BF16))
-    fwd = forward_in.reshape(2, channels, half, second)
-    back = back_part.reshape(1, channels, half, second)
+    shaped = signals.reshape(3, channels, half, second)
 
     def whole(shape):
         return pl.BlockSpec(shape, lambda i: (0,) * len(shape))
@@ -189,8 +191,7 @@
         lambda *refs: conv_kernel(block, *refs),
         grid=(channels // block,),
         in_specs=[
-            pl.BlockSpec((2, block, half, second), lambda i: (0, i, 0, 0)),
-            pl.BlockSpec((1, block, half, second), lambda i: (0, i, 0, 0)),
+            pl.BlockSpec((3, block, half, second), lambda i: (0, i, 0, 0)),
         ]
         + [whole(t.shape) for t in tables],
         out_specs=pl.BlockSpec((3, block, half, second), lambda i: (0, i, 0, 0)),
@@ -198,31 +199,99 @@
         scratch_shapes=[pltpu.VMEM((3 * block * rows, 2 * second), BF16), pltpu.VMEM((3 * block * rows, 2 * second), F32)],
         compiler_params=pltpu.CompilerParams(dimension_semantics=("arbitrary",)),
         name="hyena_conv",
-    )(fwd, back, *tables)
+    )(shaped, *tables)
     return out.reshape(3, channels, length)
 
 
+def pack_kernel(key_ref, value_ref, taps_ref, grad_ref, query_ref, out_ref):
+    block_devices, total, rows = out_ref.shape
+    per = total // 3
+    gated = key_ref[...].astype(F32) * value_ref[...].astype(F32)
+    back_in = grad_ref[...].astype(F32) * query_ref[...].astype(F32)
+    for a, values in enumerate((gated, taps_ref[...].astype(F32), back_in)):
+        out_ref[:, a * per:(a + 1) * per, :] = values.T.astype(BF16).reshape(block_devices, per, rows)
+
+
+def pack(chunk, chunks, key, value, taps, grad, query, steps=4):
+    rows, width = key.shape
+    devices = lax.psum(1, AXES)
+    per = width // (chunks * devices)
+    cols = width // (chunks * steps)
+    in_spec = pl.BlockSpec((rows, cols), lambda i: (0, chunk * steps + i))
+    return pl.pallas_call(
+        pack_kernel,
+        grid=(steps,),
+        in_specs=[in_spec] * 5,
+        out_specs=pl.BlockSpec((devices // steps, 3 * per, rows), lambda i: (i, 0, 0)),
+        out_shape=jax.ShapeDtypeStruct((devices, 3 * per, rows), BF16),
+        compiler_params=pltpu.CompilerParams(dimension_semantics=("arbitrary",)),
+        name="hyena_pack",
+    )(key, value, taps, grad, query)
+
+
+def unpack_kernel(moved_ref, query_ref, grad_ref, key_ref, value_ref, *refs):
+    mixed_ref, q_grad_ref, k_grad_ref, v_grad_ref, filter_ref = refs[-5:]
+    block_devices, total, rows = moved_ref.shape
+    per = total // 3
+
+    def part(a):
+        return moved_ref[:, a * per:(a + 1) * per, :].reshape(block_devices * per, rows).astype(F32).T
+
+    conv_back = part(0)
+    mixed_ref[...] = (query_ref[...].astype(F32) * conv_back).astype(BF16)
+    q_grad_ref[...] = (grad_ref[...].astype(F32) * conv_back).astype(BF16)
+    grad_back = part(1)
+    k_grad_ref[...] = (grad_back * value_ref[...].astype(F32)).astype(BF16)
+    v_grad_ref[...] = (grad_back * key_ref[...].astype(F32)).astype(BF16)
+    filter_ref[...] = part(2).astype(BF16)
+
+
+def unpack(chunk, chunks, moved, query, grad, key, value, previous=None, steps=4):
+    rows, width = key.shape
+    devices = moved.shape[0]
+    cols = width // (chunks * steps)
+    spec = pl.BlockSpec((rows, cols), lambda i: (0, chunk * steps + i))
+    in_specs = [pl.BlockSpec((devices // steps, moved.shape[1], rows), lambda i: (i, 0, 0))] + [spec] * 4
+    operands = [moved, query, grad, key, value]
+    aliases = {}
+    if previous is not None:
+        in_specs += [pl.BlockSpec(memory_space=pl.ANY)] * 5
+        aliases = {5 + j: j for j in range(5)}
+        operands += list(previous)
+    return pl.pallas_call(
+        unpack_kernel,
+        grid=(steps,),
+        in_specs=in_specs,
+        out_specs=[spec] * 5,
+        out_shape=[jax.ShapeDtypeStruct((rows, width), BF16)] * 5,
+        input_output_aliases=aliases,
+        compiler_params=pltpu.CompilerParams(dimension_semantics=("arbitrary",)),
+        name="hyena_unpack",
+    )(*operands)
+
+
+def from_packed(moved, count):
+    devices, total, rows = moved.shape
+    per = total // count
+    return moved.reshape(devices, count, per, rows).transpose(1, 2, 0, 3).reshape(count, per, devices * rows)
+
+
+def to_packed(cols):
+    count, per, length = cols.shape
+    devices = lax.psum(1, AXES)
+    rows = length // devices
+    return cols.reshape(count, per, devices, rows).transpose(2, 0, 1, 3).reshape(devices, count * per, rows)
+
+
 def body(q_proj, k_proj, v_proj, filter_taps, out_grad, chunks=2):
-    query = q_proj.astype(F32)
-    key = k_proj.astype(F32)
-    value = v_proj.astype(F32)
-    cotangent = out_grad.astype(F32)
-    gated = (key * value).astype(BF16)
-    back_in = (cotangent * query).astype(BF16)
-
-    width = gated.shape[1] // chunks
-    inputs = [
-        to_channels([a[:, h * width:(h + 1) * width] for a in (gated, filter_taps, back_in)]) for h in range(chunks)
-    ]
-    pieces = [to_tokens(convolve(part[:2], part[2:])) for part in inputs]
-    moved = jnp.concatenate(pieces, axis=2)
-    conv_back = moved[0].astype(F32)
-    grad_back = moved[1].astype(F32)
-    mixed = (query * conv_back).astype(BF16)
-    q_grad = (cotangent * conv_back).astype(BF16)
-    k_grad = (grad_back * value).astype(BF16)
-    v_grad = (grad_back * key).astype(BF16)
-    return (mixed, q_grad, k_grad, v_grad, moved[2])
+    outputs = None
+    packed = [pack(h, chunks, k_proj, v_proj, filter_taps, out_grad, q_proj) for h in range(chunks)]
+    for h in range(chunks):
+        arrived = lax.all_to_all(packed[h], AXES, split_axis=0, concat_axis=0, tiled=True)
+        results = convolve(from_packed(arrived, 3))
+        back = lax.all_to_all(to_packed(results), AXES, split_axis=0, concat_axis=0, tiled=True)
+        outputs = unpack(h, chunks, back, q_proj, out_grad, k_proj, v_proj, outputs)
+    return tuple(outputs)
 
 
 def solution(mesh):

time: 167 us -> 143 us (0.86)
  local copies, waits for them, and re-layouts: 40 us -> 15.3 us
  Pallas kernels: 29.4 us -> 46.3 us
  other arithmetic: 15.3 us -> 3.16 us
  starting transfers between devices: 32.4 us -> 30.4 us
  waiting for transfers between devices: 48.1 us -> 46.4 us
    pallas_call x0 -> x4, Pallas kernels: none -> 17 us  [the longest x2 8.64 us: unpack(): pl.pallas_call(unpack_kernel, grid=(steps,), in_specs=in_specs, out_specs...]
    unnamed x39 -> x4, local copies, waits for them, and re-layouts: 18.5 us -> 2.34 us
    reshape x2 -> x0, local copies, waits for them, and re-layouts: 7.19 us -> none  [to_tokens(): packed.reshape(devices, count * per_device, rows)]
    convert_element_type x3 -> x0, other arithmetic: 7.13 us -> none  [the longest x1 6.58 us: body(): v_grad = (grad_back * key).astype(BF16)]
    slice x7 -> x0, local copies, waits for them, and re-layouts: 5.92 us -> none  [the longest x4 3.74 us: body(): pieces = [to_tokens(convolve(part[:2], part[2:])) for part in inputs]]
    concatenate x2 -> x0, other arithmetic: 4.93 us -> none  [to_channels(): jnp.concatenate([a.T.reshape(devices, per_device, rows) for a in arrays],...]
    transpose x2, local copies, waits for them, and re-layouts: 3.51 us -> 7.15 us  [to_packed(): cols.reshape(count, per, devices, rows).transpose(2, 0, 1, 3)]
    all_to_all x4, starting transfers between devices: 32.4 us -> 30.4 us  [the longest x2 15.8 us: body(): lax.all_to_all(packed[h], AXES, split_axis=0, concat_axis=0, tiled=True)]
  transfers between devices with their start and end apart: 4 -> 4, of which waited for: 3 -> 3; matrix products, arithmetic and copies ran while one was open for 15% -> 11% of each run, Pallas kernels for 18% -> 27%
where the time goes in v4:
time: 143 us; the launch traced here: 142 us
  waiting for transfers between devices  46.4 us (32%)
  Pallas kernels  46.3 us (32%)
  starting transfers between devices  30.4 us (21%)
  local copies, waits for them, and re-layouts  15.3 us (11%)
  other arithmetic  3.16 us (2%)
    pallas_call x2, Pallas kernels, convolve(): pl.pallas_call(lambda *refs: conv_kernel(block, *refs), grid=(channels //...  29.3 us
    all_to_all x2, waiting for transfers between devices, body(): lax.all_to_all(to_packed(results), AXES, split_axis=0, concat_axis=0, til...  25.7 us
    all_to_all x2, waiting for transfers between devices, body(): lax.all_to_all(packed[h], AXES, split_axis=0, concat_axis=0, tiled=True)  20.8 us
    all_to_all x2, starting transfers between devices, body(): lax.all_to_all(packed[h], AXES, split_axis=0, concat_axis=0, tiled=True)  15.8 us
    all_to_all x2, starting transfers between devices, body(): lax.all_to_all(to_packed(results), AXES, split_axis=0, concat_axis=0, til...  14.6 us
    pallas_call x2, Pallas kernels, unpack(): pl.pallas_call(unpack_kernel, grid=(steps,), in_specs=in_specs, out_specs...  8.64 us
    pallas_call x2, Pallas kernels, pack(): pl.pallas_call(pack_kernel, grid=(steps,), in_specs=[in_spec] * 5, out_sp...  8.35 us
    transpose x2, local copies, waits for them, and re-layouts, to_packed(): cols.reshape(count, per, devices, rows).transpose(2, 0, 1, 3)  7.15 us
  transfers between devices with their start and end apart: 4, of which 3 were waited for; matrix products, arithmetic and copies ran while one was open for 11% of the time, Pallas kernels for 27%

profile of v4, /device:TPU:0, one launch (start us, length us, event | category | flops | bytes accessed | tf_op | source)
XLA Modules:
  0.0 142.4 jit_solution(10798375898216685672)
XLA Ops:
  0.6 4.2 %hyena_pack.3 = bf16[128,48,128]{2,1,0:T(8,128)(2,1)} custom-call(bf16[128,4096]{1,0:T(8,128)(2,1)} %key_ref.7, bf16[128,4096]{1,0:T(8,128)(2,1)} %value_ref.7, bf16[128,4096]{1,0:T(8,128)(2,1)} %taps_ref.3, bf16[128,4096]{1,0:T(8,128)(2,1)} %grad_ref.7, bf16[128,4096]{1,0:T(8,128)(2,1)} %query_ref.7), custom_call_target="tpu_custom_call" | custom-call | tf_op jit(solution)/shard_map/hyena_pack/pallas_call | solution.py:221
  4.8 11.2 %all-to-all-start.2 = ((bf16[128,48,128]{2,1,0:T(8,128)(2,1)}), bf16[128,48,128]{2,1,0:T(8,128)(2,1)S(1)}, u32[]{:S(2)}, u32[]{:S(2)}) async-start(bf16[128,48,128]{2,1,0:T(8,128)(2,1)} %hyena_pack.3), calls=%async_computation.2 | async-start | bytes 3145728 | tf_op jit(solution)/shard_map/all_to_all | solution.py:290
  16.0 4.2 %hyena_pack.2 = bf16[128,48,128]{2,1,0:T(8,128)(2,1)} custom-call(bf16[128,4096]{1,0:T(8,128)(2,1)} %key_ref.7, bf16[128,4096]{1,0:T(8,128)(2,1)} %value_ref.7, bf16[128,4096]{1,0:T(8,128)(2,1)} %taps_ref.3, bf16[128,4096]{1,0:T(8,128)(2,1)} %grad_ref.7, bf16[128,4096]{1,0:T(8,128)(2,1)} %query_ref.7), custom_call_target="tpu_custom_call" | custom-call | tf_op jit(solution)/shard_map/hyena_pack/pallas_call | solution.py:221
  20.2 20.8 %all-to-all-done.2 = bf16[128,48,128]{2,1,0:T(8,128)(2,1)S(1)} async-done(((bf16[128,48,128]{2,1,0:T(8,128)(2,1)}), bf16[128,48,128]{2,1,0:T(8,128)(2,1)S(1)}, u32[]{:S(2)}, u32[]{:S(2)}) %all-to-all-start.2) | async-done | bytes 1572896 | tf_op jit(solution)/shard_map/all_to_all | solution.py:290
  40.9 4.6 %all-to-all-start = ((bf16[128,48,128]{2,1,0:T(8,128)(2,1)}), bf16[128,48,128]{2,1,0:T(8,128)(2,1)S(1)}, u32[]{:S(2)}, u32[]{:S(2)}) async-start(bf16[128,48,128]{2,1,0:T(8,128)(2,1)} %hyena_pack.2), calls=%async_computation | async-start | bytes 3145728 | tf_op jit(solution)/shard_map/all_to_all | solution.py:290
  45.6 0.1 fusion.6
  45.7 0.5 slice_sine_fusion
  46.1 0.7 copy.18.refs_3_
  46.9 0.7 copy.17.refs_2_
  47.6 0.1 fusion.4
  47.7 0.4 fusion.20
  48.1 0.5 multiply_bitcast_fusion.1
  48.6 0.1 pad_maximum_fusion.4
  48.7 0.7 copy.16.refs_1_
  49.4 0.3 fusion.21
  49.7 0.3 sine_convert_fusion.1
  50.0 0.7 fusion.refs_6_
  50.7 0.7 fusion.2
  51.5 1.6 %copy.20 = bf16[128,48,128]{2,0,1:T(8,128)(2,1)} copy(bf16[128,48,128]{2,1,0:T(8,128)(2,1)S(1)} %all-to-all-done.2) | data formatting | bytes 3145728 | tf_op jit(solution)/shard_map/all_to_all | solution.py:290
  53.0 14.7 %hyena_conv.3 = bf16[3,16,128,128]{3,2,1,0:T(8,128)(2,1)} custom-call(bf16[3,16,128,128]{3,2,1,0:T(8,128)(2,1)} %bitcast.16, bf16[288,128]{1,0:T(8,128)(2,1)} %copy.16.refs_1_, f32[144,128]{1,0:T(8,128)} %copy.17.refs_2_, f32[144,128]{1,0:T(8,128)} %copy.18.refs_3_, bf16[256,256]{1,0:T(8,128)(2,1)} %get-tuple-element.21.refs_4_, ...), custom_call_target="tpu_custom_call" | custom-call | tf_op jit(solution)/shard_map/hyena_conv/pallas_call | solution.py:190
  67.7 3.6 %copy.24 = bf16[128,3,16,128]{3,2,1,0:T(8,128)(2,1)} copy(bf16[128,3,16,128]{3,0,2,1:T(8,128)(2,1)} %bitcast.17) | data formatting | bytes 3145728 | tf_op jit(solution)/shard_map/transpose | solution.py:283
  71.3 0.0 all-to-all-done
  71.3 9.9 %all-to-all-start.3 = ((bf16[128,48,128]{2,1,0:T(8,128)(2,1)}), bf16[128,48,128]{2,1,0:T(8,128)(2,1)S(1)}, u32[]{:S(2)}, u32[]{:S(2)}) async-start(bf16[128,48,128]{2,1,0:T(8,128)(2,1)} %bitcast.9), calls=%async_computation.3 | async-start | bytes 3145728 | tf_op jit(solution)/shard_map/all_to_all | solution.py:292
  81.2 1.5 %copy.15 = bf16[128,48,128]{2,0,1:T(8,128)(2,1)} copy(bf16[128,48,128]{2,1,0:T(8,128)(2,1)S(1)} %all-to-all-done) | data formatting | bytes 3145728 | tf_op jit(solution)/shard_map/all_to_all | solution.py:290
  82.8 14.6 %hyena_conv.2 = bf16[3,16,128,128]{3,2,1,0:T(8,128)(2,1)} custom-call(bf16[3,16,128,128]{3,2,1,0:T(8,128)(2,1)} %bitcast.14, bf16[288,128]{1,0:T(8,128)(2,1)} %copy.16.refs_1_, f32[144,128]{1,0:T(8,128)} %copy.17.refs_2_, f32[144,128]{1,0:T(8,128)} %copy.18.refs_3_, bf16[256,256]{1,0:T(8,128)(2,1)} %get-tuple-element.21.refs_4_, ...), custom_call_target="tpu_custom_call" | custom-call | tf_op jit(solution)/shard_map/hyena_conv/pallas_call | solution.py:190
  97.4 3.6 %copy.19 = bf16[128,3,16,128]{3,2,1,0:T(8,128)(2,1)} copy(bf16[128,3,16,128]{3,0,2,1:T(8,128)(2,1)} %bitcast.15) | data formatting | bytes 3145728 | tf_op jit(solution)/shard_map/transpose | solution.py:283
  101.0 5.0 %all-to-all-done.3.moved_ref = bf16[128,48,128]{2,1,0:T(8,128)(2,1)S(1)} async-done(((bf16[128,48,128]{2,1,0:T(8,128)(2,1)}), bf16[128,48,128]{2,1,0:T(8,128)(2,1)S(1)}, u32[]{:S(2)}, u32[]{:S(2)}) %all-to-all-start.3) | async-done | bytes 1572896 | tf_op jit(solution)/shard_map/all_to_all | solution.py:292
  106.0 0.0 copy-start
  106.0 1.2 copy-done
  107.2 4.6 %all-to-all-start.1 = ((bf16[128,48,128]{2,1,0:T(8,128)(2,1)}), bf16[128,48,128]{2,1,0:T(8,128)(2,1)S(1)}, u32[]{:S(2)}, u32[]{:S(2)}) async-start(bf16[128,48,128]{2,1,0:T(8,128)(2,1)} %bitcast.5), calls=%async_computation.1 | async-start | bytes 3145728 | tf_op jit(solution)/shard_map/all_to_all | solution.py:292
  111.8 4.3 %hyena_unpack.2 = (bf16[128,4096]{1,0:T(8,128)(2,1)}, bf16[128,4096]{1,0:T(8,128)(2,1)}, bf16[128,4096]{1,0:T(8,128)(2,1)}, bf16[128,4096]{1,0:T(8,128)(2,1)}, bf16[128,4096]{1,0:T(8,128)(2,1)}) custom-call(bf16[128,48,128]{2,1,0:T(8,128)(2,1)} %copy-done, bf16[128,4096]{1,0:T(8,128)(2,1)} %query_ref.7, bf16[128,4096]{1,0:T(8,128)(2,1)} %grad_ref.7, ...), custom_call_target="tpu_custom_call" | custom-call | tf_op jit(solution)/shard_map/hyena_unpack/pallas_call | solution.py:261
  116.2 20.6 %all-to-all-done.1.moved_ref = bf16[128,48,128]{2,1,0:T(8,128)(2,1)S(1)} async-done(((bf16[128,48,128]{2,1,0:T(8,128)(2,1)}), bf16[128,48,128]{2,1,0:T(8,128)(2,1)S(1)}, u32[]{:S(2)}, u32[]{:S(2)}) %all-to-all-start.1) | async-done | bytes 1572896 | tf_op jit(solution)/shard_map/all_to_all | solution.py:292
  136.8 0.0 copy-start.1
  136.8 1.2 copy-done.1
  138.0 4.3 %hyena_unpack.3 = (bf16[128,4096]{1,0:T(8,128)(2,1)}, bf16[128,4096]{1,0:T(8,128)(2,1)}, bf16[128,4096]{1,0:T(8,128)(2,1)}, bf16[128,4096]{1,0:T(8,128)(2,1)}, bf16[128,4096]{1,0:T(8,128)(2,1)}) custom-call(bf16[128,48,128]{2,1,0:T(8,128)(2,1)} %copy-done.1, ...), custom_call_target="tpu_custom_call", output_to_operand_aliasing={{0}: (5, {}), {1}: (6, {}), {2}: (7, {}), {3}: (8, {}), {4}... | custom-call | tf_op jit(solution)/shard_map/hyena_unpack/pallas_call | solution.py:261
  (1 shorter events, 0.0 us)
Async XLA Ops:
  4.8 36.1 %all-to-all-start.2 = ((bf16[128,48,128]{2,1,0:T(8,128)(2,1)}), bf16[128,48,128]{2,1,0:T(8,128)(2,1)S(1)}, u32[]{:S(2)}, u32[]{:S(2)}) async-start(bf16[128,48,128]{2,1,0:T(8,128)(2,1)} %hyena_pack.3), calls=%async_computation.2 | async-start | bytes 3145728 | tf_op jit(solution)/shard_map/all_to_all | solution.py:290
  40.9 30.3 %all-to-all-start = ((bf16[128,48,128]{2,1,0:T(8,128)(2,1)}), bf16[128,48,128]{2,1,0:T(8,128)(2,1)S(1)}, u32[]{:S(2)}, u32[]{:S(2)}) async-start(bf16[128,48,128]{2,1,0:T(8,128)(2,1)} %hyena_pack.2), calls=%async_computation | async-start | bytes 3145728 | tf_op jit(solution)/shard_map/all_to_all | solution.py:290
  71.3 34.7 %all-to-all-start.3 = ((bf16[128,48,128]{2,1,0:T(8,128)(2,1)}), bf16[128,48,128]{2,1,0:T(8,128)(2,1)S(1)}, u32[]{:S(2)}, u32[]{:S(2)}) async-start(bf16[128,48,128]{2,1,0:T(8,128)(2,1)} %bitcast.9), calls=%async_computation.3 | async-start | bytes 3145728 | tf_op jit(solution)/shard_map/all_to_all | solution.py:292
  106.0 1.2 copy-start
  107.2 29.6 %all-to-all-start.1 = ((bf16[128,48,128]{2,1,0:T(8,128)(2,1)}), bf16[128,48,128]{2,1,0:T(8,128)(2,1)S(1)}, u32[]{:S(2)}, u32[]{:S(2)}) async-start(bf16[128,48,128]{2,1,0:T(8,128)(2,1)} %bitcast.5), calls=%async_computation.1 | async-start | bytes 3145728 | tf_op jit(solution)/shard_map/all_to_all | solution.py:292
  136.8 1.2 copy-start.1

commit v5 on v4

--- a/solution.py
+++ b/solution.py
@@ -1,6 +1,7 @@
 import math
 
 import jax
+import numpy as np
 import jax.numpy as jnp
 from jax import lax
 from jax.experimental import pallas as pl
@@ -15,104 +16,38 @@
 def build_tables(first, second):
     points = first * second
     half = first // 2
-    rows_first = jnp.arange(first, dtype=jnp.int32)
-    rows_half = jnp.arange(half, dtype=jnp.int32)
-    rows_second = jnp.arange(second, dtype=jnp.int32)
-    outer_phase = rows_first[:, None] * rows_half[None, :] % first
-    outer_angle = outer_phase.astype(F32) * (2.0 * math.pi / first)
-    turn_phase = rows_first[:, None] * rows_second[None, :] % points
-    turn_angle = turn_phase.astype(F32) * (2.0 * math.pi / points)
-    inner_phase = rows_second[:, None] * rows_second[None, :] % second
-    inner_angle = inner_phase.astype(F32) * (2.0 * math.pi / second)
+    rows_first = np.arange(first)
+    rows_half = np.arange(half)
+    rows_second = np.arange(second)
+    outer_angle = (rows_first[:, None] * rows_half[None, :] % first) * (2.0 * math.pi / first)
+    turn_angle = (rows_first[:, None] * rows_second[None, :] % points) * (2.0 * math.pi / points)
+    inner_angle = (rows_second[:, None] * rows_second[None, :] % second) * (2.0 * math.pi / second)
     return (
-        jnp.cos(outer_angle).astype(BF16),
-        jnp.sin(outer_angle).astype(BF16),
-        jnp.cos(turn_angle),
-        jnp.sin(turn_angle),
-        jnp.cos(inner_angle).astype(BF16),
-        jnp.sin(inner_angle).astype(BF16),
+        np.cos(outer_angle),
+        np.sin(outer_angle),
+        np.cos(turn_angle),
+        np.sin(turn_angle),
+        np.cos(inner_angle),
+        np.sin(inner_angle),
     )
 
 
-def mm(spec, left, right):
-    return jnp.einsum(spec, left.astype(BF16), right.astype(BF16), preferred_element_type=F32)
-
-
-def forward_spectrum(tables, signal):
-    outer_cos, outer_sin, turn_cos, turn_sin, inner_cos, inner_sin = tables
-    half = outer_cos.shape[1]
-    second = inner_cos.shape[0]
-    shaped = signal.reshape(signal.shape[0], half, second)
-    real_outer = mm("kn,cnm->ckm", outer_cos, shaped)
-    imag_outer = -mm("kn,cnm->ckm", outer_sin, shaped)
-    real_turned = real_outer * turn_cos + imag_outer * turn_sin
-    imag_turned = imag_outer * turn_cos - real_outer * turn_sin
-    real_spec = mm("ckn,mn->ckm", real_turned, inner_cos) + mm("ckn,mn->ckm", imag_turned, inner_sin)
-    imag_spec = mm("ckn,mn->ckm", imag_turned, inner_cos) - mm("ckn,mn->ckm", real_turned, inner_sin)
-    return (real_spec, imag_spec)
-
-
-def inverse_signal(tables, spec_pair, scale):
-    outer_cos, outer_sin, turn_cos, turn_sin, inner_cos, inner_sin = tables
-    real_spec, imag_spec = spec_pair
-    real_inner = mm("ckn,mn->ckm", real_spec, inner_cos) - mm("ckn,mn->ckm", imag_spec, inner_sin)
-    imag_inner = mm("ckn,mn->ckm", imag_spec, inner_cos) + mm("ckn,mn->ckm", real_spec, inner_sin)
-    real_turned = (real_inner * turn_cos - imag_inner * turn_sin) * scale
-    imag_turned = (imag_inner * turn_cos + real_inner * turn_sin) * scale
-    result = mm("kn,ckm->cnm", outer_cos, real_turned) - mm("kn,ckm->cnm", outer_sin, imag_turned)
-    return result.reshape(result.shape[0], -1)
-
-
-def product(left_pair, right_pair):
+def kernel_tables(first, second, rows, scale):
+    outer_cos, outer_sin, turn_cos, turn_sin, inner_cos, inner_sin = build_tables(first, second)
+    stage_one = np.concatenate([outer_cos[:rows], -outer_sin[:rows]], axis=0)
+    forward_two = np.block([[inner_cos, -inner_sin], [inner_sin, inner_cos]])
+    inverse_two = np.block([[inner_cos, inner_sin], [-inner_sin, inner_cos]])
+    index = np.arange(rows)
+    weight = np.where((index == 0) | (index == first // 2), 1.0, np.where(index < first // 2, 2.0, 0.0))[None, :]
+    stage_last = np.concatenate([outer_cos[:rows].T * weight, -outer_sin[:rows].T * weight], axis=1) * scale
     return (
-        left_pair[0] * right_pair[0] - left_pair[1] * right_pair[1],
-        left_pair[0] * right_pair[1] + left_pair[1] * right_pair[0],
+        jnp.asarray(stage_one.astype(BF16)),
+        jnp.asarray(turn_cos[:rows].astype(np.float32)),
+        jnp.asarray(turn_sin[:rows].astype(np.float32)),
+        jnp.asarray(forward_two.astype(BF16)),
+        jnp.asarray(inverse_two.astype(BF16)),
+        jnp.asarray(stage_last.astype(BF16)),
     )
-
-
-def product_conj(left_pair, right_pair):
-    return (
-        left_pair[0] * right_pair[0] + left_pair[1] * right_pair[1],
-        left_pair[1] * right_pair[0] - left_pair[0] * right_pair[1],
-    )
-
-
-def to_channels(arrays):
-    rows, width = arrays[0].shape
-    devices = lax.psum(1, AXES)
-    per_device = width // devices
-    packed = jnp.concatenate([a.T.reshape(devices, per_device, rows) for a in arrays], axis=1)
-    moved = lax.all_to_all(packed, AXES, split_axis=0, concat_axis=0, tiled=True)
-    moved = moved.reshape(devices, len(arrays), per_device, rows).transpose(1, 2, 0, 3)
-    return moved.reshape(len(arrays), per_device, devices * rows)
-
-
-def to_tokens(cols):
-    count, per_device, length = cols.shape
-    devices = lax.psum(1, AXES)
-    rows = length // devices
-    packed = cols.reshape(count, per_device, devices, rows).transpose(2, 0, 1, 3)
-    moved = lax.all_to_all(packed.reshape(devices, count * per_device, rows), AXES, split_axis=0, concat_axis=0, tiled=True)
-    moved = moved.reshape(devices, count, per_device, rows).transpose(1, 3, 0, 2)
-    return moved.reshape(count, rows, devices * per_device)
-
-
-def kernel_tables(first, second, rows):
-    outer_cos, outer_sin, turn_cos, turn_sin, inner_cos, inner_sin = build_tables(first, second)
-    stage_one = jnp.concatenate([outer_cos[:rows], -outer_sin[:rows]], axis=0)
-    forward_two = jnp.concatenate(
-        [jnp.concatenate([inner_cos, -inner_sin], axis=1), jnp.concatenate([inner_sin, inner_cos], axis=1)], axis=0
-    )
-    inverse_two = jnp.concatenate(
-        [jnp.concatenate([inner_cos, inner_sin], axis=1), jnp.concatenate([-inner_sin, inner_cos], axis=1)], axis=0
-    )
-    index = jnp.arange(rows)
-    weight = jnp.where((index == 0) | (index == first // 2), 1.0, jnp.where(index < first // 2, 2.0, 0.0))
-    weight = weight.astype(F32)[None, :]
-    stage_last = jnp.concatenate(
-        [outer_cos[:rows].T.astype(F32) * weight, -outer_sin[:rows].T.astype(F32) * weight], axis=1
-    )
-    return (stage_one, turn_cos[:rows], turn_sin[:rows], forward_two, inverse_two, stage_last)
 
 
 def conv_kernel(block, sig_ref, one_ref, tc_ref, ts_ref, two_ref, inv_ref, last_ref, out_ref, turned_ref, spec_ref):
@@ -180,8 +115,7 @@
     scale = 1.0 / (math.sqrt(length) * points)
     if rows is None:
         rows = min(first, -(-(half + 1) // 16) * 16)
-    stage_one, turn_c, turn_s, forward_two, inverse_two, stage_last = kernel_tables(first, second, rows)
-    tables = (stage_one, turn_c, turn_s, forward_two, inverse_two, (stage_last.astype(F32) * scale).astype(BF16))
+    tables = kernel_tables(first, second, rows, scale)
     shaped = signals.reshape(3, channels, half, second)
 
     def whole(shape):

time: 143 us -> 137 us (0.958)
  waiting for transfers between devices: 46.4 us -> 51.7 us
  starting transfers between devices: 30.4 us -> 25.1 us
  other arithmetic: 3.16 us -> 0 us
  local copies, waits for them, and re-layouts: 15.3 us -> 12.6 us
    all_to_all x2, starting transfers between devices: 14.6 us -> 9.28 us  [body(): lax.all_to_all(to_packed(results), AXES, split_axis=0, concat_axis=0, til...]
    all_to_all x2, waiting for transfers between devices: 20.8 us -> 25.9 us  [body(): lax.all_to_all(packed[h], AXES, split_axis=0, concat_axis=0, tiled=True)]
    slice x2 -> x0, local copies, waits for them, and re-layouts: 1.46 us -> none  [the longest x1 0.73 us: kernel_tables(): turn_cos[:rows]]
  transfers between devices with their start and end apart: 4 -> 4, of which waited for: 3 -> 4; matrix products, arithmetic and copies ran while one was open for 11% -> 8% of each run, Pallas kernels for 27% -> 28%
where the time goes in v5:
time: 137 us; the launch traced here: 136 us
  waiting for transfers between devices  51.7 us (38%)
  Pallas kernels  46.4 us (34%)
  starting transfers between devices  25.1 us (18%)
  local copies, waits for them, and re-layouts  12.6 us (9%)
    pallas_call x2, Pallas kernels, convolve(): pl.pallas_call(lambda *refs: conv_kernel(block, *refs), grid=(channels //...  29.4 us
    all_to_all x2, waiting for transfers between devices, body(): lax.all_to_all(packed[h], AXES, split_axis=0, concat_axis=0, tiled=True)  25.9 us
    all_to_all x2, waiting for transfers between devices, body(): lax.all_to_all(to_packed(results), AXES, split_axis=0, concat_axis=0, til...  25.8 us
    all_to_all x2, starting transfers between devices, body(): lax.all_to_all(packed[h], AXES, split_axis=0, concat_axis=0, tiled=True)  15.8 us
    all_to_all x2, starting transfers between devices, body(): lax.all_to_all(to_packed(results), AXES, split_axis=0, concat_axis=0, til...  9.28 us
    pallas_call x2, Pallas kernels, unpack(): pl.pallas_call(unpack_kernel, grid=(steps,), in_specs=in_specs, out_specs...  8.64 us
    pallas_call x2, Pallas kernels, pack(): pl.pallas_call(pack_kernel, grid=(steps,), in_specs=[in_spec] * 5, out_sp...  8.36 us
    transpose x2, local copies, waits for them, and re-layouts, to_packed(): cols.reshape(count, per, devices, rows).transpose(2, 0, 1, 3)  7.15 us
  transfers between devices with their start and end apart: 4, of which 4 were waited for; matrix products, arithmetic and copies ran while one was open for 8% of the time, Pallas kernels for 28%

profile of v5, /device:TPU:0, one launch (start us, length us, event | category | flops | bytes accessed | tf_op | source)
XLA Modules:
  0.0 136.4 jit_solution(16844230072585238517)
XLA Ops:
  0.6 4.2 %hyena_pack.3 = bf16[128,48,128]{2,1,0:T(8,128)(2,1)} custom-call(bf16[128,4096]{1,0:T(8,128)(2,1)} %key_ref.7, bf16[128,4096]{1,0:T(8,128)(2,1)} %value_ref.7, bf16[128,4096]{1,0:T(8,128)(2,1)} %taps_ref.3, bf16[128,4096]{1,0:T(8,128)(2,1)} %grad_ref.7, bf16[128,4096]{1,0:T(8,128)(2,1)} %query_ref.7), custom_call_target="tpu_custom_call" | custom-call | tf_op jit(solution)/shard_map/hyena_pack/pallas_call | solution.py:155
  4.8 11.2 %all-to-all-start.2 = ((bf16[128,48,128]{2,1,0:T(8,128)(2,1)}), bf16[128,48,128]{2,1,0:T(8,128)(2,1)S(1)}, u32[]{:S(2)}, u32[]{:S(2)}) async-start(bf16[128,48,128]{2,1,0:T(8,128)(2,1)} %hyena_pack.3), calls=%async_computation.2 | async-start | bytes 3145728 | tf_op jit(solution)/shard_map/all_to_all | solution.py:224
  16.0 4.2 %hyena_pack.2 = bf16[128,48,128]{2,1,0:T(8,128)(2,1)} custom-call(bf16[128,4096]{1,0:T(8,128)(2,1)} %key_ref.7, bf16[128,4096]{1,0:T(8,128)(2,1)} %value_ref.7, bf16[128,4096]{1,0:T(8,128)(2,1)} %taps_ref.3, bf16[128,4096]{1,0:T(8,128)(2,1)} %grad_ref.7, bf16[128,4096]{1,0:T(8,128)(2,1)} %query_ref.7), custom_call_target="tpu_custom_call" | custom-call | tf_op jit(solution)/shard_map/hyena_pack/pallas_call | solution.py:155
  20.2 20.8 %all-to-all-done.2 = bf16[128,48,128]{2,1,0:T(8,128)(2,1)S(1)} async-done(((bf16[128,48,128]{2,1,0:T(8,128)(2,1)}), bf16[128,48,128]{2,1,0:T(8,128)(2,1)S(1)}, u32[]{:S(2)}, u32[]{:S(2)}) %all-to-all-start.2) | async-done | bytes 1572896 | tf_op jit(solution)/shard_map/all_to_all | solution.py:224
  41.0 4.6 %all-to-all-start = ((bf16[128,48,128]{2,1,0:T(8,128)(2,1)}), bf16[128,48,128]{2,1,0:T(8,128)(2,1)S(1)}, u32[]{:S(2)}, u32[]{:S(2)}) async-start(bf16[128,48,128]{2,1,0:T(8,128)(2,1)} %hyena_pack.2), calls=%async_computation | async-start | bytes 3145728 | tf_op jit(solution)/shard_map/all_to_all | solution.py:224
  45.6 1.6 %copy.29 = bf16[128,48,128]{2,0,1:T(8,128)(2,1)} copy(bf16[128,48,128]{2,1,0:T(8,128)(2,1)S(1)} %all-to-all-done.2) | data formatting | bytes 3145728 | tf_op jit(solution)/shard_map/all_to_all | solution.py:224
  47.2 14.7 %hyena_conv.3 = bf16[3,16,128,128]{3,2,1,0:T(8,128)(2,1)} custom-call(bf16[3,16,128,128]{3,2,1,0:T(8,128)(2,1)} %bitcast.12, bf16[288,128]{1,0:T(8,128)(2,1)} %constant.12.clone.refs_1_, f32[144,128]{1,0:T(8,128)} %constant.13.clone.refs_2_, f32[144,128]{1,0:T(8,128)} %constant.14.clone.refs_3_, bf16[256,256]{1,0:T(8,128)(2,1)} %constant.15.clone.refs_4_, ...), custom_call_target="tpu_custom_call" | custom-call | tf_op jit(solution)/shard_map/hyena_conv/pallas_call | solution.py:124
  61.9 3.6 %copy.30 = bf16[128,3,16,128]{3,2,1,0:T(8,128)(2,1)} copy(bf16[128,3,16,128]{3,0,2,1:T(8,128)(2,1)} %bitcast.13) | data formatting | bytes 3145728 | tf_op jit(solution)/shard_map/transpose | solution.py:217
  65.4 5.2 %all-to-all-done = bf16[128,48,128]{2,1,0:T(8,128)(2,1)S(1)} async-done(((bf16[128,48,128]{2,1,0:T(8,128)(2,1)}), bf16[128,48,128]{2,1,0:T(8,128)(2,1)S(1)}, u32[]{:S(2)}, u32[]{:S(2)}) %all-to-all-start) | async-done | bytes 1572896 | tf_op jit(solution)/shard_map/all_to_all | solution.py:224
  70.6 4.6 %all-to-all-start.3 = ((bf16[128,48,128]{2,1,0:T(8,128)(2,1)}), bf16[128,48,128]{2,1,0:T(8,128)(2,1)S(1)}, u32[]{:S(2)}, u32[]{:S(2)}) async-start(bf16[128,48,128]{2,1,0:T(8,128)(2,1)} %bitcast.7), calls=%async_computation.3 | async-start | bytes 3145728 | tf_op jit(solution)/shard_map/all_to_all | solution.py:226
  75.2 1.6 %copy.27 = bf16[128,48,128]{2,0,1:T(8,128)(2,1)} copy(bf16[128,48,128]{2,1,0:T(8,128)(2,1)S(1)} %all-to-all-done) | data formatting | bytes 3145728 | tf_op jit(solution)/shard_map/all_to_all | solution.py:224
  76.8 14.7 %hyena_conv.2 = bf16[3,16,128,128]{3,2,1,0:T(8,128)(2,1)} custom-call(bf16[3,16,128,128]{3,2,1,0:T(8,128)(2,1)} %bitcast.10, bf16[288,128]{1,0:T(8,128)(2,1)} %constant.12.clone.refs_1_, f32[144,128]{1,0:T(8,128)} %constant.13.clone.refs_2_, f32[144,128]{1,0:T(8,128)} %constant.14.clone.refs_3_, bf16[256,256]{1,0:T(8,128)(2,1)} %constant.15.clone.refs_4_, ...), custom_call_target="tpu_custom_call" | custom-call | tf_op jit(solution)/shard_map/hyena_conv/pallas_call | solution.py:124
  91.5 3.6 %copy.28 = bf16[128,3,16,128]{3,2,1,0:T(8,128)(2,1)} copy(bf16[128,3,16,128]{3,0,2,1:T(8,128)(2,1)} %bitcast.11) | data formatting | bytes 3145728 | tf_op jit(solution)/shard_map/transpose | solution.py:217
  95.1 5.1 %all-to-all-done.3.moved_ref = bf16[128,48,128]{2,1,0:T(8,128)(2,1)S(1)} async-done(((bf16[128,48,128]{2,1,0:T(8,128)(2,1)}), bf16[128,48,128]{2,1,0:T(8,128)(2,1)S(1)}, u32[]{:S(2)}, u32[]{:S(2)}) %all-to-all-start.3) | async-done | bytes 1572896 | tf_op jit(solution)/shard_map/all_to_all | solution.py:226
  100.2 0.0 copy-start
  100.2 1.1 copy-done
  101.4 4.6 %all-to-all-start.1 = ((bf16[128,48,128]{2,1,0:T(8,128)(2,1)}), bf16[128,48,128]{2,1,0:T(8,128)(2,1)S(1)}, u32[]{:S(2)}, u32[]{:S(2)}) async-start(bf16[128,48,128]{2,1,0:T(8,128)(2,1)} %bitcast.3), calls=%async_computation.1 | async-start | bytes 3145728 | tf_op jit(solution)/shard_map/all_to_all | solution.py:226
  106.0 4.3 %hyena_unpack.2 = (bf16[128,4096]{1,0:T(8,128)(2,1)}, bf16[128,4096]{1,0:T(8,128)(2,1)}, bf16[128,4096]{1,0:T(8,128)(2,1)}, bf16[128,4096]{1,0:T(8,128)(2,1)}, bf16[128,4096]{1,0:T(8,128)(2,1)}) custom-call(bf16[128,48,128]{2,1,0:T(8,128)(2,1)} %copy-done, bf16[128,4096]{1,0:T(8,128)(2,1)} %query_ref.7, bf16[128,4096]{1,0:T(8,128)(2,1)} %grad_ref.7, ...), custom_call_target="tpu_custom_call" | custom-call | tf_op jit(solution)/shard_map/hyena_unpack/pallas_call | solution.py:195
  110.3 20.6 %all-to-all-done.1.moved_ref = bf16[128,48,128]{2,1,0:T(8,128)(2,1)S(1)} async-done(((bf16[128,48,128]{2,1,0:T(8,128)(2,1)}), bf16[128,48,128]{2,1,0:T(8,128)(2,1)S(1)}, u32[]{:S(2)}, u32[]{:S(2)}) %all-to-all-start.1) | async-done | bytes 1572896 | tf_op jit(solution)/shard_map/all_to_all | solution.py:226
  131.0 0.0 copy-start.1
  131.0 1.1 copy-done.1
  132.1 4.3 %hyena_unpack.3 = (bf16[128,4096]{1,0:T(8,128)(2,1)}, bf16[128,4096]{1,0:T(8,128)(2,1)}, bf16[128,4096]{1,0:T(8,128)(2,1)}, bf16[128,4096]{1,0:T(8,128)(2,1)}, bf16[128,4096]{1,0:T(8,128)(2,1)}) custom-call(bf16[128,48,128]{2,1,0:T(8,128)(2,1)} %copy-done.1, ...), custom_call_target="tpu_custom_call", output_to_operand_aliasing={{0}: (5, {}), {1}: (6, {}), {2}: (7, {}), {3}: (8, {}), {4}... | custom-call | tf_op jit(solution)/shard_map/hyena_unpack/pallas_call | solution.py:195
Async XLA Ops:
  4.8 36.1 %all-to-all-start.2 = ((bf16[128,48,128]{2,1,0:T(8,128)(2,1)}), bf16[128,48,128]{2,1,0:T(8,128)(2,1)S(1)}, u32[]{:S(2)}, u32[]{:S(2)}) async-start(bf16[128,48,128]{2,1,0:T(8,128)(2,1)} %hyena_pack.3), calls=%async_computation.2 | async-start | bytes 3145728 | tf_op jit(solution)/shard_map/all_to_all | solution.py:224
  41.0 29.6 %all-to-all-start = ((bf16[128,48,128]{2,1,0:T(8,128)(2,1)}), bf16[128,48,128]{2,1,0:T(8,128)(2,1)S(1)}, u32[]{:S(2)}, u32[]{:S(2)}) async-start(bf16[128,48,128]{2,1,0:T(8,128)(2,1)} %hyena_pack.2), calls=%async_computation | async-start | bytes 3145728 | tf_op jit(solution)/shard_map/all_to_all | solution.py:224
  70.6 29.6 %all-to-all-start.3 = ((bf16[128,48,128]{2,1,0:T(8,128)(2,1)}), bf16[128,48,128]{2,1,0:T(8,128)(2,1)S(1)}, u32[]{:S(2)}, u32[]{:S(2)}) async-start(bf16[128,48,128]{2,1,0:T(8,128)(2,1)} %bitcast.7), calls=%async_computation.3 | async-start | bytes 3145728 | tf_op jit(solution)/shard_map/all_to_all | solution.py:226
  100.2 1.2 copy-start
  101.4 29.6 %all-to-all-start.1 = ((bf16[128,48,128]{2,1,0:T(8,128)(2,1)}), bf16[128,48,128]{2,1,0:T(8,128)(2,1)S(1)}, u32[]{:S(2)}, u32[]{:S(2)}) async-start(bf16[128,48,128]{2,1,0:T(8,128)(2,1)} %bitcast.3), calls=%async_computation.1 | async-start | bytes 3145728 | tf_op jit(solution)/shard_map/all_to_all | solution.py:226
  131.0 1.2 copy-start.1

commit v6 on v5

--- a/solution.py
+++ b/solution.py
@@ -146,7 +146,7 @@
         out_ref[:, a * per:(a + 1) * per, :] = values.T.astype(BF16).reshape(block_devices, per, rows)
 
 
-def pack(chunk, chunks, key, value, taps, grad, query, steps=4):
+def pack(chunk, chunks, key, value, taps, grad, query, steps=2):
     rows, width = key.shape
     devices = lax.psum(1, AXES)
     per = width // (chunks * devices)
@@ -180,7 +180,7 @@
     filter_ref[...] = part(2).astype(BF16)
 
 
-def unpack(chunk, chunks, moved, query, grad, key, value, previous=None, steps=4):
+def unpack(chunk, chunks, moved, query, grad, key, value, previous=None, steps=2):
     rows, width = key.shape
     devices = moved.shape[0]
     cols = width // (chunks * steps)

time: 137 us -> 135 us (0.985)
  Pallas kernels: 46.4 us -> 41.7 us
  waiting for transfers between devices: 51.7 us -> 54.1 us
    pallas_call x2, Pallas kernels: 8.36 us -> 5.78 us  [pack(): pl.pallas_call(pack_kernel, grid=(steps,), in_specs=[in_spec] * 5, out_sp...]
    pallas_call x2, Pallas kernels: 8.64 us -> 6.59 us  [unpack(): pl.pallas_call(unpack_kernel, grid=(steps,), in_specs=in_specs, out_specs...]
  transfers between devices with their start and end apart: 4 -> 4, of which waited for: 4 -> 4; matrix products, arithmetic and copies ran while one was open for 8% -> 8% of each run, Pallas kernels for 28% -> 26%
where the time goes in v6:
time: 135 us; the launch traced here: 134 us
  waiting for transfers between devices  54.1 us (40%)
  Pallas kernels  41.7 us (31%)
  starting transfers between devices  25.1 us (19%)
  local copies, waits for them, and re-layouts  12.6 us (9%)
    pallas_call x2, Pallas kernels, convolve(): pl.pallas_call(lambda *refs: conv_kernel(block, *refs), grid=(channels //...  29.3 us
    all_to_all x2, waiting for transfers between devices, body(): lax.all_to_all(packed[h], AXES, split_axis=0, concat_axis=0, tiled=True)  27.2 us
    all_to_all x2, waiting for transfers between devices, body(): lax.all_to_all(to_packed(results), AXES, split_axis=0, concat_axis=0, til...  26.9 us
    all_to_all x2, starting transfers between devices, body(): lax.all_to_all(packed[h], AXES, split_axis=0, concat_axis=0, tiled=True)  15.8 us
    all_to_all x2, starting transfers between devices, body(): lax.all_to_all(to_packed(results), AXES, split_axis=0, concat_axis=0, til...  9.28 us
    transpose x2, local copies, waits for them, and re-layouts, to_packed(): cols.reshape(count, per, devices, rows).transpose(2, 0, 1, 3)  7.15 us
    pallas_call x2, Pallas kernels, unpack(): pl.pallas_call(unpack_kernel, grid=(steps,), in_specs=in_specs, out_specs...  6.59 us
    pallas_call x2, Pallas kernels, pack(): pl.pallas_call(pack_kernel, grid=(steps,), in_specs=[in_spec] * 5, out_sp...  5.78 us
  transfers between devices with their start and end apart: 4, of which 4 were waited for; matrix products, arithmetic and copies ran while one was open for 8% of the time, Pallas kernels for 26%

profile of v6, /device:TPU:0, one launch (start us, length us, event | category | flops | bytes accessed | tf_op | source)
XLA Modules:
  0.0 134.2 jit_solution(12178497602767070885)
XLA Ops:
  0.6 2.9 %hyena_pack.3 = bf16[128,48,128]{2,1,0:T(8,128)(2,1)} custom-call(bf16[128,4096]{1,0:T(8,128)(2,1)} %key_ref.7, bf16[128,4096]{1,0:T(8,128)(2,1)} %value_ref.7, bf16[128,4096]{1,0:T(8,128)(2,1)} %taps_ref.3, bf16[128,4096]{1,0:T(8,128)(2,1)} %grad_ref.7, bf16[128,4096]{1,0:T(8,128)(2,1)} %query_ref.7), custom_call_target="tpu_custom_call" | custom-call | tf_op jit(solution)/shard_map/hyena_pack/pallas_call | solution.py:155
  3.5 11.2 %all-to-all-start.2 = ((bf16[128,48,128]{2,1,0:T(8,128)(2,1)}), bf16[128,48,128]{2,1,0:T(8,128)(2,1)S(1)}, u32[]{:S(2)}, u32[]{:S(2)}) async-start(bf16[128,48,128]{2,1,0:T(8,128)(2,1)} %hyena_pack.3), calls=%async_computation.2 | async-start | bytes 3145728 | tf_op jit(solution)/shard_map/all_to_all | solution.py:224
  14.7 2.9 %hyena_pack.2 = bf16[128,48,128]{2,1,0:T(8,128)(2,1)} custom-call(bf16[128,4096]{1,0:T(8,128)(2,1)} %key_ref.7, bf16[128,4096]{1,0:T(8,128)(2,1)} %value_ref.7, bf16[128,4096]{1,0:T(8,128)(2,1)} %taps_ref.3, bf16[128,4096]{1,0:T(8,128)(2,1)} %grad_ref.7, bf16[128,4096]{1,0:T(8,128)(2,1)} %query_ref.7), custom_call_target="tpu_custom_call" | custom-call | tf_op jit(solution)/shard_map/hyena_pack/pallas_call | solution.py:155
  17.6 22.1 %all-to-all-done.2 = bf16[128,48,128]{2,1,0:T(8,128)(2,1)S(1)} async-done(((bf16[128,48,128]{2,1,0:T(8,128)(2,1)}), bf16[128,48,128]{2,1,0:T(8,128)(2,1)S(1)}, u32[]{:S(2)}, u32[]{:S(2)}) %all-to-all-start.2) | async-done | bytes 1572896 | tf_op jit(solution)/shard_map/all_to_all | solution.py:224
  39.7 4.6 %all-to-all-start = ((bf16[128,48,128]{2,1,0:T(8,128)(2,1)}), bf16[128,48,128]{2,1,0:T(8,128)(2,1)S(1)}, u32[]{:S(2)}, u32[]{:S(2)}) async-start(bf16[128,48,128]{2,1,0:T(8,128)(2,1)} %hyena_pack.2), calls=%async_computation | async-start | bytes 3145728 | tf_op jit(solution)/shard_map/all_to_all | solution.py:224
  44.3 1.6 %copy.29 = bf16[128,48,128]{2,0,1:T(8,128)(2,1)} copy(bf16[128,48,128]{2,1,0:T(8,128)(2,1)S(1)} %all-to-all-done.2) | data formatting | bytes 3145728 | tf_op jit(solution)/shard_map/all_to_all | solution.py:224
  45.9 14.7 %hyena_conv.3 = bf16[3,16,128,128]{3,2,1,0:T(8,128)(2,1)} custom-call(bf16[3,16,128,128]{3,2,1,0:T(8,128)(2,1)} %bitcast.12, bf16[288,128]{1,0:T(8,128)(2,1)} %constant.12.clone.refs_1_, f32[144,128]{1,0:T(8,128)} %constant.13.clone.refs_2_, f32[144,128]{1,0:T(8,128)} %constant.14.clone.refs_3_, bf16[256,256]{1,0:T(8,128)(2,1)} %constant.15.clone.refs_4_, ...), custom_call_target="tpu_custom_call" | custom-call | tf_op jit(solution)/shard_map/hyena_conv/pallas_call | solution.py:124
  60.6 3.6 %copy.30 = bf16[128,3,16,128]{3,2,1,0:T(8,128)(2,1)} copy(bf16[128,3,16,128]{3,0,2,1:T(8,128)(2,1)} %bitcast.13) | data formatting | bytes 3145728 | tf_op jit(solution)/shard_map/transpose | solution.py:217
  64.1 5.2 %all-to-all-done = bf16[128,48,128]{2,1,0:T(8,128)(2,1)S(1)} async-done(((bf16[128,48,128]{2,1,0:T(8,128)(2,1)}), bf16[128,48,128]{2,1,0:T(8,128)(2,1)S(1)}, u32[]{:S(2)}, u32[]{:S(2)}) %all-to-all-start) | async-done | bytes 1572896 | tf_op jit(solution)/shard_map/all_to_all | solution.py:224
  69.3 4.6 %all-to-all-start.3 = ((bf16[128,48,128]{2,1,0:T(8,128)(2,1)}), bf16[128,48,128]{2,1,0:T(8,128)(2,1)S(1)}, u32[]{:S(2)}, u32[]{:S(2)}) async-start(bf16[128,48,128]{2,1,0:T(8,128)(2,1)} %bitcast.7), calls=%async_computation.3 | async-start | bytes 3145728 | tf_op jit(solution)/shard_map/all_to_all | solution.py:226
  73.9 1.6 %copy.27 = bf16[128,48,128]{2,0,1:T(8,128)(2,1)} copy(bf16[128,48,128]{2,1,0:T(8,128)(2,1)S(1)} %all-to-all-done) | data formatting | bytes 3145728 | tf_op jit(solution)/shard_map/all_to_all | solution.py:224
  75.5 14.7 %hyena_conv.2 = bf16[3,16,128,128]{3,2,1,0:T(8,128)(2,1)} custom-call(bf16[3,16,128,128]{3,2,1,0:T(8,128)(2,1)} %bitcast.10, bf16[288,128]{1,0:T(8,128)(2,1)} %constant.12.clone.refs_1_, f32[144,128]{1,0:T(8,128)} %constant.13.clone.refs_2_, f32[144,128]{1,0:T(8,128)} %constant.14.clone.refs_3_, bf16[256,256]{1,0:T(8,128)(2,1)} %constant.15.clone.refs_4_, ...), custom_call_target="tpu_custom_call" | custom-call | tf_op jit(solution)/shard_map/hyena_conv/pallas_call | solution.py:124
  90.2 3.6 %copy.28 = bf16[128,3,16,128]{3,2,1,0:T(8,128)(2,1)} copy(bf16[128,3,16,128]{3,0,2,1:T(8,128)(2,1)} %bitcast.11) | data formatting | bytes 3145728 | tf_op jit(solution)/shard_map/transpose | solution.py:217
  93.8 5.1 %all-to-all-done.3.moved_ref = bf16[128,48,128]{2,1,0:T(8,128)(2,1)S(1)} async-done(((bf16[128,48,128]{2,1,0:T(8,128)(2,1)}), bf16[128,48,128]{2,1,0:T(8,128)(2,1)S(1)}, u32[]{:S(2)}, u32[]{:S(2)}) %all-to-all-start.3) | async-done | bytes 1572896 | tf_op jit(solution)/shard_map/all_to_all | solution.py:226
  98.9 0.0 copy-start
  98.9 1.1 copy-done
  100.1 4.6 %all-to-all-start.1 = ((bf16[128,48,128]{2,1,0:T(8,128)(2,1)}), bf16[128,48,128]{2,1,0:T(8,128)(2,1)S(1)}, u32[]{:S(2)}, u32[]{:S(2)}) async-start(bf16[128,48,128]{2,1,0:T(8,128)(2,1)} %bitcast.3), calls=%async_computation.1 | async-start | bytes 3145728 | tf_op jit(solution)/shard_map/all_to_all | solution.py:226
  104.7 3.3 %hyena_unpack.2 = (bf16[128,4096]{1,0:T(8,128)(2,1)}, bf16[128,4096]{1,0:T(8,128)(2,1)}, bf16[128,4096]{1,0:T(8,128)(2,1)}, bf16[128,4096]{1,0:T(8,128)(2,1)}, bf16[128,4096]{1,0:T(8,128)(2,1)}) custom-call(bf16[128,48,128]{2,1,0:T(8,128)(2,1)} %copy-done, bf16[128,4096]{1,0:T(8,128)(2,1)} %query_ref.7, bf16[128,4096]{1,0:T(8,128)(2,1)} %grad_ref.7, ...), custom_call_target="tpu_custom_call" | custom-call | tf_op jit(solution)/shard_map/hyena_unpack/pallas_call | solution.py:195
  108.0 21.7 %all-to-all-done.1.moved_ref = bf16[128,48,128]{2,1,0:T(8,128)(2,1)S(1)} async-done(((bf16[128,48,128]{2,1,0:T(8,128)(2,1)}), bf16[128,48,128]{2,1,0:T(8,128)(2,1)S(1)}, u32[]{:S(2)}, u32[]{:S(2)}) %all-to-all-start.1) | async-done | bytes 1572896 | tf_op jit(solution)/shard_map/all_to_all | solution.py:226
  129.7 0.0 copy-start.1
  129.7 1.1 copy-done.1
  130.8 3.3 %hyena_unpack.3 = (bf16[128,4096]{1,0:T(8,128)(2,1)}, bf16[128,4096]{1,0:T(8,128)(2,1)}, bf16[128,4096]{1,0:T(8,128)(2,1)}, bf16[128,4096]{1,0:T(8,128)(2,1)}, bf16[128,4096]{1,0:T(8,128)(2,1)}) custom-call(bf16[128,48,128]{2,1,0:T(8,128)(2,1)} %copy-done.1, ...), custom_call_target="tpu_custom_call", output_to_operand_aliasing={{0}: (5, {}), {1}: (6, {}), {2}: (7, {}), {3}: (8, {}), {4}... | custom-call | tf_op jit(solution)/shard_map/hyena_unpack/pallas_call | solution.py:195
Async XLA Ops:
  3.5 36.1 %all-to-all-start.2 = ((bf16[128,48,128]{2,1,0:T(8,128)(2,1)}), bf16[128,48,128]{2,1,0:T(8,128)(2,1)S(1)}, u32[]{:S(2)}, u32[]{:S(2)}) async-start(bf16[128,48,128]{2,1,0:T(8,128)(2,1)} %hyena_pack.3), calls=%async_computation.2 | async-start | bytes 3145728 | tf_op jit(solution)/shard_map/all_to_all | solution.py:224
  39.7 29.6 %all-to-all-start = ((bf16[128,48,128]{2,1,0:T(8,128)(2,1)}), bf16[128,48,128]{2,1,0:T(8,128)(2,1)S(1)}, u32[]{:S(2)}, u32[]{:S(2)}) async-start(bf16[128,48,128]{2,1,0:T(8,128)(2,1)} %hyena_pack.2), calls=%async_computation | async-start | bytes 3145728 | tf_op jit(solution)/shard_map/all_to_all | solution.py:224
  69.3 29.6 %all-to-all-start.3 = ((bf16[128,48,128]{2,1,0:T(8,128)(2,1)}), bf16[128,48,128]{2,1,0:T(8,128)(2,1)S(1)}, u32[]{:S(2)}, u32[]{:S(2)}) async-start(bf16[128,48,128]{2,1,0:T(8,128)(2,1)} %bitcast.7), calls=%async_computation.3 | async-start | bytes 3145728 | tf_op jit(solution)/shard_map/all_to_all | solution.py:226
  98.9 1.2 copy-start
  100.1 29.6 %all-to-all-start.1 = ((bf16[128,48,128]{2,1,0:T(8,128)(2,1)}), bf16[128,48,128]{2,1,0:T(8,128)(2,1)S(1)}, u32[]{:S(2)}, u32[]{:S(2)}) async-start(bf16[128,48,128]{2,1,0:T(8,128)(2,1)} %bitcast.3), calls=%async_computation.1 | async-start | bytes 3145728 | tf_op jit(solution)/shard_map/all_to_all | solution.py:226
  129.7 1.2 copy-start.1

commit v7 on v6

--- a/solution.py
+++ b/solution.py
@@ -217,6 +217,23 @@
     return cols.reshape(count, per, devices, rows).transpose(2, 0, 1, 3).reshape(devices, count * per, rows)
 
 
+def unpack_first(moved, query, grad, key, value):
+    devices, total, rows = moved.shape
+    per = total // 3
+    cols = devices * per
+    parts = moved.reshape(devices, 3, per, rows).transpose(1, 3, 0, 2).reshape(3, rows, cols).astype(F32)
+    conv_back, grad_back = parts[0], parts[1]
+    values = (
+        query[:, :cols].astype(F32) * conv_back,
+        grad[:, :cols].astype(F32) * conv_back,
+        grad_back * value[:, :cols].astype(F32),
+        grad_back * key[:, :cols].astype(F32),
+        parts[2],
+    )
+    empty = jnp.zeros(query.shape, BF16)
+    return [lax.dynamic_update_slice(empty, v.astype(BF16), (0, 0)) for v in values]
+
+
 def body(q_proj, k_proj, v_proj, filter_taps, out_grad, chunks=2):
     outputs = None
     packed = [pack(h, chunks, k_proj, v_proj, filter_taps, out_grad, q_proj) for h in range(chunks)]
@@ -224,7 +241,10 @@
         arrived = lax.all_to_all(packed[h], AXES, split_axis=0, concat_axis=0, tiled=True)
         results = convolve(from_packed(arrived, 3))
         back = lax.all_to_all(to_packed(results), AXES, split_axis=0, concat_axis=0, tiled=True)
-        outputs = unpack(h, chunks, back, q_proj, out_grad, k_proj, v_proj, outputs)
+        if h == 0:
+            outputs = unpack_first(back, q_proj, out_grad, k_proj, v_proj)
+        else:
+            outputs = unpack(h, chunks, back, q_proj, out_grad, k_proj, v_proj, outputs)
     return tuple(outputs)
 
 

time: 135 us -> 133 us (0.985)
  local copies, waits for them, and re-layouts: 12.6 us -> 22.6 us
  waiting for transfers between devices: 54.1 us -> 44.1 us
  Pallas kernels: 41.7 us -> 38.5 us
    all_to_all x2, waiting for transfers between devices: 26.9 us -> 16.9 us  [body(): lax.all_to_all(to_packed(results), AXES, split_axis=0, concat_axis=0, til...]
    dynamic_update_slice x0 -> x5, local copies, waits for them, and re-layouts: none -> 6.53 us  [unpack_first(): lax.dynamic_update_slice(empty, v.astype(BF16), (0, 0))]
    transpose x2 -> x1, local copies, waits for them, and re-layouts: 7.15 us -> 3.56 us  [to_packed(): cols.reshape(count, per, devices, rows).transpose(2, 0, 1, 3)]
    reshape x0 -> x1, local copies, waits for them, and re-layouts: none -> 3.59 us  [to_packed(): cols.reshape(count, per, devices, rows).transpose(2, 0, 1, 3)]
    pallas_call x2 -> x1, Pallas kernels: 6.59 us -> 3.34 us  [unpack(): pl.pallas_call(unpack_kernel, grid=(steps,), in_specs=in_specs, out_specs...]
    squeeze x0 -> x2, local copies, waits for them, and re-layouts: none -> 3.01 us  [unpack_first(): conv_back, grad_back = (parts[0], parts[1])]
    unnamed x4 -> x10, local copies, waits for them, and re-layouts: 2.3 us -> 0.63 us
  transfers between devices with their start and end apart: 4 -> 4, of which waited for: 4 -> 4; matrix products, arithmetic and copies ran while one was open for 8% -> 17% of each run, Pallas kernels for 26% -> 24%
where the time goes in v7:
time: 133 us
  waiting for transfers between devices  44.1 us (33%)
  Pallas kernels  38.5 us (29%)
  starting transfers between devices  26.2 us (20%)
  local copies, waits for them, and re-layouts  22.6 us (17%)
    pallas_call x2, Pallas kernels, convolve(): pl.pallas_call(lambda *refs: conv_kernel(block, *refs), grid=(channels //...  29.3 us
    all_to_all x2, waiting for transfers between devices, body(): lax.all_to_all(packed[h], AXES, split_axis=0, concat_axis=0, tiled=True)  27.2 us
    all_to_all x2, waiting for transfers between devices, body(): lax.all_to_all(to_packed(results), AXES, split_axis=0, concat_axis=0, til...  16.9 us
    all_to_all x2, starting transfers between devices, body(): lax.all_to_all(packed[h], AXES, split_axis=0, concat_axis=0, tiled=True)  15.8 us
    all_to_all x2, starting transfers between devices, body(): lax.all_to_all(to_packed(results), AXES, split_axis=0, concat_axis=0, til...  10.3 us
    dynamic_update_slice x5, local copies, waits for them, and re-layouts, unpack_first(): lax.dynamic_update_slice(empty, v.astype(BF16), (0, 0))  6.53 us
    pallas_call x2, Pallas kernels, pack(): pl.pallas_call(pack_kernel, grid=(steps,), in_specs=[in_spec] * 5, out_sp...  5.79 us
    reshape x1, local copies, waits for them, and re-layouts, to_packed(): cols.reshape(count, per, devices, rows).transpose(2, 0, 1, 3)  3.59 us
  transfers between devices with their start and end apart: 4, of which 4 were waited for; matrix products, arithmetic and copies ran while one was open for 17% of the time, Pallas kernels for 24%

profile of v7, /device:TPU:0, one launch (start us, length us, event | category | flops | bytes accessed | tf_op | source)
XLA Modules:
  0.0 132.6 jit_solution(12595398513213509899)
XLA Ops:
  0.6 2.9 %hyena_pack.3 = bf16[128,48,128]{2,1,0:T(8,128)(2,1)} custom-call(bf16[128,4096]{1,0:T(8,128)(2,1)} %key_ref.5, bf16[128,4096]{1,0:T(8,128)(2,1)} %value_ref.5, bf16[128,4096]{1,0:T(8,128)(2,1)} %taps_ref.3, bf16[128,4096]{1,0:T(8,128)(2,1)} %grad_ref.5, bf16[128,4096]{1,0:T(8,128)(2,1)} %query_ref.5), custom_call_target="tpu_custom_call" | custom-call | tf_op jit(solution)/shard_map/hyena_pack/pallas_call | solution.py:155
  3.5 11.2 %all-to-all-start.2 = ((bf16[128,48,128]{2,1,0:T(8,128)(2,1)}), bf16[128,48,128]{2,1,0:T(8,128)(2,1)S(1)}, u32[]{:S(2)}, u32[]{:S(2)}) async-start(bf16[128,48,128]{2,1,0:T(8,128)(2,1)} %hyena_pack.3), calls=%async_computation.2 | async-start | bytes 3145728 | tf_op jit(solution)/shard_map/all_to_all | solution.py:241
  14.7 2.9 %hyena_pack.2 = bf16[128,48,128]{2,1,0:T(8,128)(2,1)} custom-call(bf16[128,4096]{1,0:T(8,128)(2,1)} %key_ref.5, bf16[128,4096]{1,0:T(8,128)(2,1)} %value_ref.5, bf16[128,4096]{1,0:T(8,128)(2,1)} %taps_ref.3, bf16[128,4096]{1,0:T(8,128)(2,1)} %grad_ref.5, bf16[128,4096]{1,0:T(8,128)(2,1)} %query_ref.5), custom_call_target="tpu_custom_call" | custom-call | tf_op jit(solution)/shard_map/hyena_pack/pallas_call | solution.py:155
  17.6 22.1 %all-to-all-done.2 = bf16[128,48,128]{2,1,0:T(8,128)(2,1)S(1)} async-done(((bf16[128,48,128]{2,1,0:T(8,128)(2,1)}), bf16[128,48,128]{2,1,0:T(8,128)(2,1)S(1)}, u32[]{:S(2)}, u32[]{:S(2)}) %all-to-all-start.2) | async-done | bytes 1572896 | tf_op jit(solution)/shard_map/all_to_all | solution.py:241
  39.7 4.6 %all-to-all-start = ((bf16[128,48,128]{2,1,0:T(8,128)(2,1)}), bf16[128,48,128]{2,1,0:T(8,128)(2,1)S(1)}, u32[]{:S(2)}, u32[]{:S(2)}) async-start(bf16[128,48,128]{2,1,0:T(8,128)(2,1)} %hyena_pack.2), calls=%async_computation | async-start | bytes 3145728 | tf_op jit(solution)/shard_map/all_to_all | solution.py:241
  44.3 1.6 %copy.32 = bf16[128,48,128]{2,0,1:T(8,128)(2,1)} copy(bf16[128,48,128]{2,1,0:T(8,128)(2,1)S(1)} %all-to-all-done.2) | data formatting | bytes 3145728 | tf_op jit(solution)/shard_map/all_to_all | solution.py:241
  45.9 14.7 %hyena_conv.3 = bf16[3,16,128,128]{3,2,1,0:T(8,128)(2,1)} custom-call(bf16[3,16,128,128]{3,2,1,0:T(8,128)(2,1)} %bitcast.21, bf16[288,128]{1,0:T(8,128)(2,1)} %constant.6.clone.refs_1_, f32[144,128]{1,0:T(8,128)} %constant.16.clone.refs_2_, f32[144,128]{1,0:T(8,128)} %constant.17.clone.refs_3_, bf16[256,256]{1,0:T(8,128)(2,1)} %constant.18.clone.refs_4_, ...), custom_call_target="tpu_custom_call" | custom-call | tf_op jit(solution)/shard_map/hyena_conv/pallas_call | solution.py:124
  60.6 3.6 %copy.33 = bf16[128,48,128]{2,1,0:T(8,128)(2,1)} copy(bf16[128,48,128]{2,0,1:T(8,128)(2,1)} %bitcast.22) | data formatting | bytes 3145728 | tf_op jit(solution)/shard_map/reshape | solution.py:217
  64.2 5.1 %all-to-all-done = bf16[128,48,128]{2,1,0:T(8,128)(2,1)S(1)} async-done(((bf16[128,48,128]{2,1,0:T(8,128)(2,1)}), bf16[128,48,128]{2,1,0:T(8,128)(2,1)S(1)}, u32[]{:S(2)}, u32[]{:S(2)}) %all-to-all-start) | async-done | bytes 1572896 | tf_op jit(solution)/shard_map/all_to_all | solution.py:241
  69.3 4.6 %all-to-all-start.3 = ((bf16[128,48,128]{2,1,0:T(8,128)(2,1)}), bf16[128,48,128]{2,1,0:T(8,128)(2,1)S(1)}, u32[]{:S(2)}, u32[]{:S(2)}) async-start(bf16[128,48,128]{2,1,0:T(8,128)(2,1)} %copy.33), calls=%async_computation.3 | async-start | bytes 3145728 | tf_op jit(solution)/shard_map/all_to_all | solution.py:243
  73.9 1.5 %copy.30 = bf16[128,48,128]{2,0,1:T(8,128)(2,1)} copy(bf16[128,48,128]{2,1,0:T(8,128)(2,1)S(1)} %all-to-all-done) | data formatting | bytes 3145728 | tf_op jit(solution)/shard_map/all_to_all | solution.py:241
  75.5 14.7 %hyena_conv.2 = bf16[3,16,128,128]{3,2,1,0:T(8,128)(2,1)} custom-call(bf16[3,16,128,128]{3,2,1,0:T(8,128)(2,1)} %bitcast.19, bf16[288,128]{1,0:T(8,128)(2,1)} %constant.6.clone.refs_1_, f32[144,128]{1,0:T(8,128)} %constant.16.clone.refs_2_, f32[144,128]{1,0:T(8,128)} %constant.17.clone.refs_3_, bf16[256,256]{1,0:T(8,128)(2,1)} %constant.18.clone.refs_4_, ...), custom_call_target="tpu_custom_call" | custom-call | tf_op jit(solution)/shard_map/hyena_conv/pallas_call | solution.py:124
  90.1 3.6 %copy.31 = bf16[128,3,16,128]{3,2,1,0:T(8,128)(2,1)} copy(bf16[128,3,16,128]{3,0,2,1:T(8,128)(2,1)} %bitcast.20) | data formatting | bytes 3145728 | tf_op jit(solution)/shard_map/transpose | solution.py:217
  93.7 5.2 %all-to-all-done.3 = bf16[128,48,128]{2,1,0:T(8,128)(2,1)S(1)} async-done(((bf16[128,48,128]{2,1,0:T(8,128)(2,1)}), bf16[128,48,128]{2,1,0:T(8,128)(2,1)S(1)}, u32[]{:S(2)}, u32[]{:S(2)}) %all-to-all-start.3) | async-done | bytes 1572896 | tf_op jit(solution)/shard_map/all_to_all | solution.py:243
  98.9 5.7 %all-to-all-start.1 = ((bf16[128,48,128]{2,1,0:T(8,128)(2,1)}), bf16[128,48,128]{2,1,0:T(8,128)(2,1)}, u32[]{:S(2)}, u32[]{:S(2)}) async-start(bf16[128,48,128]{2,1,0:T(8,128)(2,1)} %bitcast.3), calls=%async_computation.1 | async-start | bytes 3145728 | tf_op jit(solution)/shard_map/all_to_all | solution.py:243
  104.7 1.0 copy.38
  105.7 1.1 fusion
  106.8 1.3 copy.36
  108.1 0.0 copy-start
  108.1 0.0 copy-start.1
  108.1 1.7 %copy.34 = f32[128,2048]{1,0:T(8,128)S(1)} copy(f32[128,2048]{0,1:T(8,128)} %bitcast.23) | data formatting | bytes 2097152 | tf_op jit(solution)/shard_map/squeeze | solution.py:225
  109.8 0.0 copy-start.4
  109.8 2.2 %dynamic_update_slice.19.refs_4_ = bf16[128,4096]{1,0:T(8,128)(2,1)} pad(bf16[128,2048]{1,0:T(8,128)(2,1)} %copy.38, bf16[]{:T(256)} %constant.7.clone.1), padding=0_0x0_2048 | pad | bytes 1572866 | tf_op jit(solution)/shard_map/dynamic_update_slice | solution.py:234
  112.0 0.0 copy-done
  112.0 0.0 copy-done.1
  112.1 0.0 copy-done.4
  112.1 0.0 copy-start.3
  112.1 0.3 multiply_convert_fusion
  112.3 0.0 copy-start.2
  112.4 1.1 dynamic_update_slice.18.refs_3_
  113.4 0.0 copy-done.3
  113.4 0.6 copy-done.2
  114.1 0.3 multiply_convert_fusion.2
  114.3 1.1 dynamic_update_slice.16.refs_1_
  115.4 1.1 dynamic_update_slice.17.refs_2_
  116.5 1.1 dynamic_update_slice.15.refs_0_
  117.6 11.7 %all-to-all-done.1.moved_ref = bf16[128,48,128]{2,1,0:T(8,128)(2,1)} async-done(((bf16[128,48,128]{2,1,0:T(8,128)(2,1)}), bf16[128,48,128]{2,1,0:T(8,128)(2,1)}, u32[]{:S(2)}, u32[]{:S(2)}) %all-to-all-start.1) | async-done | bytes 1572896 | tf_op jit(solution)/shard_map/all_to_all | solution.py:243
  129.2 3.3 %hyena_unpack.1 = (bf16[128,4096]{1,0:T(8,128)(2,1)}, bf16[128,4096]{1,0:T(8,128)(2,1)}, bf16[128,4096]{1,0:T(8,128)(2,1)}, bf16[128,4096]{1,0:T(8,128)(2,1)}, bf16[128,4096]{1,0:T(8,128)(2,1)}) custom-call(bf16[128,48,128]{2,1,0:T(8,128)(2,1)} %all-to-all-done.1.moved_ref, ...), custom_call_target="tpu_custom_call", output_to_operand_aliasing={{0}: (5, {}), {1}: (6, {}), {2}: (7, {}), {3}: (8, {}), {4}... | custom-call | tf_op jit(solution)/shard_map/hyena_unpack/pallas_call | solution.py:195
  (1 shorter events, 0.0 us)
Async XLA Ops:
  3.5 36.1 %all-to-all-start.2 = ((bf16[128,48,128]{2,1,0:T(8,128)(2,1)}), bf16[128,48,128]{2,1,0:T(8,128)(2,1)S(1)}, u32[]{:S(2)}, u32[]{:S(2)}) async-start(bf16[128,48,128]{2,1,0:T(8,128)(2,1)} %hyena_pack.3), calls=%async_computation.2 | async-start | bytes 3145728 | tf_op jit(solution)/shard_map/all_to_all | solution.py:241
  39.7 29.6 %all-to-all-start = ((bf16[128,48,128]{2,1,0:T(8,128)(2,1)}), bf16[128,48,128]{2,1,0:T(8,128)(2,1)S(1)}, u32[]{:S(2)}, u32[]{:S(2)}) async-start(bf16[128,48,128]{2,1,0:T(8,128)(2,1)} %hyena_pack.2), calls=%async_computation | async-start | bytes 3145728 | tf_op jit(solution)/shard_map/all_to_all | solution.py:241
  69.3 29.6 %all-to-all-start.3 = ((bf16[128,48,128]{2,1,0:T(8,128)(2,1)}), bf16[128,48,128]{2,1,0:T(8,128)(2,1)S(1)}, u32[]{:S(2)}, u32[]{:S(2)}) async-start(bf16[128,48,128]{2,1,0:T(8,128)(2,1)} %copy.33), calls=%async_computation.3 | async-start | bytes 3145728 | tf_op jit(solution)/shard_map/all_to_all | solution.py:243
  98.9 30.3 %all-to-all-start.1 = ((bf16[128,48,128]{2,1,0:T(8,128)(2,1)}), bf16[128,48,128]{2,1,0:T(8,128)(2,1)}, u32[]{:S(2)}, u32[]{:S(2)}) async-start(bf16[128,48,128]{2,1,0:T(8,128)(2,1)} %bitcast.3), calls=%async_computation.1 | async-start | bytes 3145728 | tf_op jit(solution)/shard_map/all_to_all | solution.py:243
  108.1 3.9 %copy-start = (bf16[128,4096]{1,0:T(8,128)(2,1)S(1)}, bf16[128,4096]{1,0:T(8,128)(2,1)}, u32[]{:S(2)}) copy-start(bf16[128,4096]{1,0:T(8,128)(2,1)} %key_ref.5) | copy-start | bytes 3145732
  108.1 3.9 %copy-start.1 = (bf16[128,4096]{1,0:T(8,128)(2,1)S(1)}, bf16[128,4096]{1,0:T(8,128)(2,1)}, u32[]{:S(2)}) copy-start(bf16[128,4096]{1,0:T(8,128)(2,1)} %value_ref.5) | copy-start | bytes 3145732
  109.8 2.2 %copy-start.4 = (f32[128,2048]{1,0:T(8,128)S(1)}, f32[128,2048]{1,0:T(8,128)}, u32[]{:S(2)}) copy-start(f32[128,2048]{1,0:T(8,128)} %copy.36) | copy-start | bytes 3145732
  112.1 1.4 %copy-start.3 = (bf16[128,4096]{1,0:T(8,128)(2,1)S(1)}, bf16[128,4096]{1,0:T(8,128)(2,1)}, u32[]{:S(2)}) copy-start(bf16[128,4096]{1,0:T(8,128)(2,1)} %query_ref.5) | copy-start | bytes 3145732
  112.3 1.7 %copy-start.2 = (bf16[128,4096]{1,0:T(8,128)(2,1)S(1)}, bf16[128,4096]{1,0:T(8,128)(2,1)}, u32[]{:S(2)}) copy-start(bf16[128,4096]{1,0:T(8,128)(2,1)} %grad_ref.5) | copy-start | bytes 3145732
